TPU v7x, 512 devices: a whole 4x8x8 slice. The times are simulated.
512 devices in a mesh: own: 64 (over z, y), rep: 8 (over x, core).
Axes of the slice: x: 4, y: 8, z: 8, core: 2. Of those that a mesh axis runs over, the one named last changes fastest.
Arguments:
- tokens: bfloat16 [65536, 2560], P(('own', 'rep')), may hold values from -6 to 6
- cotangent: bfloat16 [65536, 2560], P(('own', 'rep')), may hold values from -6 to 6
- route: int32 [65536, 6], P(('own', 'rep')), may hold values from 0 to 159, all different within a row; in each aligned block of 128 rows (0 to 127, 128 to 255, ...) at most 6 rows name the same one
- gate_index: int32 [65536, 6], P(('own', 'rep')), may hold values from 0 to 255
- gate_table: float32 [256], replicated, may hold values from 0.1 to 1
- w_gate: bfloat16 [16384, 2560], P(('own', 'rep')), may hold values from -0.125 to 0.125
- w_up: bfloat16 [16384, 2560], P(('own', 'rep')), may hold values from -0.125 to 0.125
- w_down: bfloat16 [16384, 2560], P(('own', 'rep')), may hold values from -0.1875 to 0.1875
Outputs:
- grad_tokens: bfloat16 [65536, 2560], P(('own', 'rep'))
- grad_w_gate: float32 [16384, 2560], P(('own', 'rep'))
- grad_w_up: float32 [16384, 2560], P(('own', 'rep'))
- grad_w_down: float32 [16384, 2560], P(('own', 'rep'))
Inputs may be any that keep to these rules, and one draw needn't show every extreme that they name: `route`: each row names 6 different experts. Among the rows of one device no expert is named by more than 6 rows, and in some device some expert is named by exactly 6.
All inputs are finite; a program needn't handle non-finite values.
Results may differ from a plain program's by a relative error of at most 0.015.
Values may be sent and summed in bfloat16 or wider, within the bound.
No kernel may reach another device: no remote copies, remote signals or barrier semaphores. Data moves between devices by JAX's collectives and lax.ppermute only.
A program may use at most 64 MiB of HBM per device.

v0:
```python
import jax
import jax.numpy as jnp
from jax import lax
from jax.sharding import PartitionSpec as P

SPLIT = 4
CAP = 6


def silu_parts(pre_gate):
    sigmoid_value = jax.nn.sigmoid(pre_gate)
    return (pre_gate * sigmoid_value, sigmoid_value * (1.0 + pre_gate * (1.0 - sigmoid_value)))


def panel_terms(rows_x, rows_cot, panel_gate, panel_up, panel_down):
    pre_gate = jnp.dot(rows_x, panel_gate.T, preferred_element_type=jnp.float32)
    pre_up = jnp.dot(rows_x, panel_up.T, preferred_element_type=jnp.float32)
    active, slope_value = silu_parts(pre_gate)
    hidden = (active * pre_up).astype(jnp.bfloat16)
    hidden_delta = jnp.dot(rows_cot, panel_down.T, preferred_element_type=jnp.float32)
    gate_delta = (hidden_delta * pre_up * slope_value).astype(jnp.bfloat16)
    up_delta = (hidden_delta * active).astype(jnp.bfloat16)
    grad_rows = jnp.dot(gate_delta, panel_gate, preferred_element_type=jnp.float32) + jnp.dot(
        up_delta, panel_up, preferred_element_type=jnp.float32
    )
    grad_gate = jnp.dot(gate_delta.T, rows_x, preferred_element_type=jnp.float32)
    grad_up = jnp.dot(up_delta.T, rows_x, preferred_element_type=jnp.float32)
    grad_down = jnp.dot(hidden.T, rows_cot, preferred_element_type=jnp.float32)
    return (grad_rows, grad_gate, grad_up, grad_down)


def per_device(tokens, cotangent, route, gate_index, gate_table, w_gate, w_up, w_down):
    owners = lax.axis_size("own")
    experts_here = owners // SPLIT
    tok_count = tokens.shape[0]
    model_width = tokens.shape[1]
    choices_each = route.shape[1]
    table_hits = (
        gate_index[:, :, None] == jnp.arange(gate_table.shape[0], dtype=jnp.int32)[None, None, :]
    ).astype(jnp.float32)
    gate_values = jnp.sum(table_hits * gate_table[None, None, :], axis=2).reshape(-1)
    is_named = (
        route.reshape(-1)[:, None] == jnp.arange(experts_here, dtype=jnp.int32)[None, :]
    ).astype(jnp.int32)
    earlier = jnp.cumsum(is_named, axis=0) - is_named
    slot_hits = (
        is_named[:, :, None]
        * (earlier[:, :, None] == jnp.arange(CAP, dtype=jnp.int32)[None, None, :]).astype(jnp.int32)
    ).astype(jnp.float32)
    slot_hits = slot_hits.reshape(tok_count * choices_each, experts_here * CAP)
    select = slot_hits.reshape(tok_count, choices_each, experts_here * CAP).sum(axis=1)
    slot_gate = jnp.dot(
        gate_values, slot_hits, precision=lax.Precision.HIGHEST, preferred_element_type=jnp.float32
    )
    picker = select.astype(jnp.bfloat16)
    sent_x = jnp.dot(picker.T, tokens, preferred_element_type=jnp.float32).astype(jnp.bfloat16)
    sent_dy = jnp.dot(picker.T, cotangent, preferred_element_type=jnp.float32)
    sent_cot = (slot_gate[:, None] * sent_dy).astype(jnp.bfloat16)

    def fan_out(slot_rows):
        spread = jnp.broadcast_to(
            slot_rows.reshape(experts_here, 1, CAP, model_width),
            (experts_here, SPLIT, CAP, model_width),
        )
        return spread.reshape(owners, CAP, model_width)

    got_x, got_cot = (
        lax.all_to_all(fan_out(sent_x), "own", split_axis=0, concat_axis=0, tiled=True),
        lax.all_to_all(fan_out(sent_cot), "own", split_axis=0, concat_axis=0, tiled=True),
    )
    rows_x = got_x.reshape(owners * CAP, model_width)
    rows_cot = got_cot.reshape(owners * CAP, model_width)
    full_gate, full_up, full_down = (
        lax.all_gather(w_gate, "rep", axis=0, tiled=True),
        lax.all_gather(w_up, "rep", axis=0, tiled=True),
        lax.all_gather(w_down, "rep", axis=0, tiled=True),
    )
    grad_rows, grad_gate, grad_up, grad_down = panel_terms(
        rows_x, rows_cot, full_gate, full_up, full_down
    )
    block_rows = grad_rows.astype(jnp.bfloat16).reshape(owners, CAP, model_width)
    returned = lax.all_to_all(block_rows, "own", split_axis=0, concat_axis=0, tiled=True)
    per_slot = (
        returned.astype(jnp.float32)
        .reshape(experts_here, SPLIT, CAP, model_width)
        .sum(axis=1)
        .reshape(experts_here * CAP, model_width)
    )
    grad_tokens = jnp.dot(
        select, per_slot, precision=lax.Precision.HIGHEST, preferred_element_type=jnp.float32
    ).astype(jnp.bfloat16)
    stacked = jnp.stack([grad_gate, grad_up, grad_down]).astype(jnp.bfloat16).astype(jnp.float32)
    totals_all = lax.psum(stacked.astype(jnp.bfloat16), "rep").astype(jnp.float32)
    rows_each = stacked.shape[1] // lax.axis_size("rep")
    shares = lax.dynamic_slice_in_dim(totals_all, lax.axis_index("rep") * rows_each, rows_each, 1)
    return (grad_tokens, shares[0], shares[1], shares[2])


def solution(mesh):
    return jax.shard_map(
        per_device,
        mesh=mesh,
        in_specs=(
            P(("own", "rep"), None),
            P(("own", "rep"), None),
            P(("own", "rep"), None),
            P(("own", "rep"), None),
            P(),
            P(("own", "rep"), None),
            P(("own", "rep"), None),
            P(("own", "rep"), None),
        ),
        out_specs=(
            P(("own", "rep"), None),
            P(("own", "rep"), None),
            P(("own", "rep"), None),
            P(("own", "rep"), None),
        ),
        check_vma=False,
    )
```

profile of v0, /device:TPU:6, one launch (start us, length us, event | category | flops | bytes accessed | tf_op | source)
XLA Modules:
  0.0 343.7 jit_solution(16061698377593412336)
XLA Ops:
  7.2 0.9 copy.23
  8.0 0.1 eq.74
  8.2 0.1 eq.78
  8.3 1.7 reduce-window.6
  10.0 0.3 slice_reduce_fusion
  10.5 8.2 %eq.83 = s32[128,6,96]{1,0,2:T(8,128)} reshape(s32[768,16,6]{0,2,1:T(8,128)S(1)} %eq.82) | data formatting | bytes 589824 | tf_op jit(solution)/shard_map/eq | solution.py:48
  18.8 8.2 %mul.53 = s32[128,6,96]{1,0,2:T(8,128)} reshape(s32[768,16,6]{0,2,1:T(8,128)S(1)} %mul.52) | data formatting | bytes 589824 | tf_op jit(solution)/shard_map/mul | solution.py:47
  27.2 0.3 select_reduce_fusion
  27.5 0.1 copy.26
  27.6 0.1 reshape.136
  27.8 0.3 convolution_bitcast_fusion
  28.1 6.5 %convert_reduce_fusion = f32[128,96]{0,1:T(8,128)S(1)} fusion(s32[128,6,96]{1,0,2:T(8,128)} %mul.53, s32[128,6,96]{1,0,2:T(8,128)} %eq.83, s32[96]{0:T(128)S(1)} %eq.85), kind=kLoop, calls=%fused_computation | loop fusion | flops 282624 | bytes 639360 | tf_op jit(solution)/shard_map/reduce_sum | solution.py:51
  34.6 0.3 fusion.4
  34.8 0.2 broadcast_in_dim.8
  35.0 1.7 broadcast_in_dim.9
  36.7 16.6 %all-to-all-start = ((bf16[64,6,2560]{2,1,0:T(8,128)(2,1)}), bf16[64,6,2560]{2,1,0:T(8,128)(2,1)S(1)}, u32[]{:S(2)}, u32[]{:S(2)}) async-start(bf16[64,6,2560]{2,1,0:T(8,128)(2,1)} %bitcast.58), calls=%async_computation | async-start | bytes 5242880 | tf_op jit(solution)/shard_map/all_to_all | solution.py:69
  53.4 0.7 all-gather.6.cloned.1.call-update
  54.1 0.7 all-gather.8.cloned.1.call-update
  54.8 2.2 convolution_convert_fusion.4
  57.0 2.0 broadcast_in_dim.10
  59.0 58.6 %all-to-all-done = bf16[64,6,2560]{2,1,0:T(8,128)(2,1)S(1)} async-done(((bf16[64,6,2560]{2,1,0:T(8,128)(2,1)}), bf16[64,6,2560]{2,1,0:T(8,128)(2,1)S(1)}, u32[]{:S(2)}, u32[]{:S(2)}) %all-to-all-start) | async-done | bytes 1966112 | tf_op jit(solution)/shard_map/all_to_all | solution.py:69
  117.7 2.8 broadcast_in_dim.11
  120.4 20.7 %all-to-all-start.1 = ((bf16[64,6,2560]{2,1,0:T(8,128)(2,1)}), bf16[64,6,2560]{2,1,0:T(8,128)(2,1)}, u32[]{:S(2)}, u32[]{:S(2)}) async-start(bf16[64,6,2560]{2,1,0:T(8,128)(2,1)} %bitcast.59), calls=%async_computation.1 | async-start | bytes 5242880 | tf_op jit(solution)/shard_map/all_to_all | solution.py:68
  141.2 0.2 all-gather.4.cloned.1.call-start
  141.4 0.5 all-gather.4.cloned.1.call-update
  141.9 2.1 reshape.127
  144.0 61.1 %all-to-all-done.1 = bf16[64,6,2560]{2,1,0:T(8,128)(2,1)} async-done(((bf16[64,6,2560]{2,1,0:T(8,128)(2,1)}), bf16[64,6,2560]{2,1,0:T(8,128)(2,1)}, u32[]{:S(2)}, u32[]{:S(2)}) %all-to-all-start.1) | async-done | bytes 1966112 | tf_op jit(solution)/shard_map/all_to_all | solution.py:68
  205.1 2.8 reshape.129
  207.9 2.0 fusion.13
  210.0 2.8 fusion.14
  212.7 2.7 multiply_convert_fusion.1
  215.5 1.9 fusion.1
  217.4 0.7 fusion.15
  218.1 0.6 copy-done.3
  218.7 2.0 fusion
  220.7 4.1 %reshape.130 = bf16[64,6,2560]{2,1,0:T(8,128)(2,1)} reshape(bf16[384,2560]{1,0:T(8,128)(2,1)} %fusion) | data formatting | bytes 3932160 | tf_op jit(solution)/shard_map/reshape | solution.py:81
  224.9 19.0 %all-to-all-start.2 = ((bf16[64,6,2560]{2,1,0:T(8,128)(2,1)}), bf16[64,6,2560]{2,1,0:T(8,128)(2,1)}, u32[]{:S(2)}, u32[]{:S(2)}) async-start(bf16[64,6,2560]{2,1,0:T(8,128)(2,1)} %reshape.130), calls=%async_computation.2 | async-start | bytes 5242880 | tf_op jit(solution)/shard_map/all_to_all | solution.py:82
  243.9 0.9 fusion.2
  244.8 0.7 copy-done.1
  245.5 0.9 fusion.3
  246.4 0.4 copy-done.2
  246.8 2.1 pad_maximum_fusion
  248.9 81.6 %all-reduce.2.cloned.1.call-done = bf16[3,256,2560]{2,1,0:T(8,128)(2,1)} async-done(((bf16[3,256,2560]{2,1,0:T(8,128)(2,1)}), bf16[3,256,2560]{2,1,0:T(8,128)(2,1)}) %all-reduce.2.cloned.1.call-update) | async-done | bytes 3932176 | tf_op jit(solution)/shard_map/psum | solution.py:93
  330.5 1.1 dynamic-slice_convert_fusion
  331.6 1.0 slice_bitcast_fusion
  332.6 2.4 convert_reduce_fusion.1
  335.0 0.1 reshape.133
  335.1 2.1 convolution_convert_fusion.3
  (31 shorter events, 0.6 us)
Async XLA Ops:
  7.2 27.4 %copy-start = (bf16[128,2560]{1,0:T(8,128)(2,1)S(1)}, bf16[128,2560]{1,0:T(8,128)(2,1)}, u32[]{:S(2)}) copy-start(bf16[128,2560]{1,0:T(8,128)(2,1)} %param.9) | copy-start | bytes 1966084
  18.8 8.4 %copy-start.6 = (s32[128,6]{0,1:T(8,128)S(1)}, s32[128,6]{0,1:T(8,128)}, u32[]{:S(2)}) copy-start(s32[128,6]{0,1:T(8,128)} %param.11) | copy-start | bytes 9220
  18.8 8.4 %copy-start.7 = (f32[256]{0:T(256)S(1)}, f32[256]{0:T(256)}, u32[]{:S(2)}) copy-start(f32[256]{0:T(256)} %param.12) | copy-start | bytes 3076
  36.7 80.9 %all-to-all-start = ((bf16[64,6,2560]{2,1,0:T(8,128)(2,1)}), bf16[64,6,2560]{2,1,0:T(8,128)(2,1)S(1)}, u32[]{:S(2)}, u32[]{:S(2)}) async-start(bf16[64,6,2560]{2,1,0:T(8,128)(2,1)} %bitcast.58), calls=%async_computation | async-start | bytes 5242880 | tf_op jit(solution)/shard_map/all_to_all | solution.py:69
  53.3 154.6 %all-gather.6.cloned.1.call-start = ((), (), s32[]{:S(2)}) async-start(), calls=%async_computation.4 | async-start | bytes 1474560 | tf_op jit(solution)/shard_map/all_gather | solution.py:75
  54.1 155.9 %all-gather.8.cloned.1.call-start = ((), (), s32[]{:S(2)}) async-start(), calls=%async_computation.5 | async-start | bytes 1474560 | tf_op jit(solution)/shard_map/all_gather | solution.py:74
  120.4 84.7 %all-to-all-start.1 = ((bf16[64,6,2560]{2,1,0:T(8,128)(2,1)}), bf16[64,6,2560]{2,1,0:T(8,128)(2,1)}, u32[]{:S(2)}, u32[]{:S(2)}) async-start(bf16[64,6,2560]{2,1,0:T(8,128)(2,1)} %bitcast.59), calls=%async_computation.1 | async-start | bytes 5242880 | tf_op jit(solution)/shard_map/all_to_all | solution.py:68
  141.2 71.6 %all-gather.4.cloned.1.call-start = ((), (), s32[]{:S(2)}) async-start(), calls=%async_computation.3 | async-start | bytes 1474560 | tf_op jit(solution)/shard_map/all_gather | solution.py:76
  215.4 1.9 copy-start.4
  217.4 1.3 copy-start.3
  224.9 107.7 %all-to-all-start.2 = ((bf16[64,6,2560]{2,1,0:T(8,128)(2,1)}), bf16[64,6,2560]{2,1,0:T(8,128)(2,1)}, u32[]{:S(2)}, u32[]{:S(2)}) async-start(bf16[64,6,2560]{2,1,0:T(8,128)(2,1)} %reshape.130), calls=%async_computation.2 | async-start | bytes 5242880 | tf_op jit(solution)/shard_map/all_to_all | solution.py:82
  243.9 86.6 %all-reduce.2.cloned.1.call-start = ((), (), s32[]{:S(2)}) async-start(), calls=%async_computation.6 | async-start | bytes 7864320 | tf_op jit(solution)/shard_map/psum | solution.py:93
  243.9 1.5 copy-start.1
  243.9 1.6 copy-start.5
  245.5 1.3 copy-start.2
Sparse Core Ops, SparseCore 0:
  56.3 28.3 all-gather.5
  86.8 29.1 all-gather.7
  144.1 28.0 all-gather.3
  249.0 81.3 all-reduce.1
where the time goes:
time: 347 us; the launch traced here: 344 us
  waiting for transfers between devices  203 us (59%)
  starting transfers between devices  56.6 us (16%)
  local copies, waits for them, and re-layouts  36.9 us (11%)
  matrix products  18.7 us (5%)
  other arithmetic  14.3 us (4%)
  between operations  14 us (4%)
    psum x1, waiting for transfers between devices, per_device(): lax.psum(stacked.astype(jnp.bfloat16), 'rep').astype(jnp.float32)  81.6 us
    all_to_all x1, waiting for transfers between devices, per_device(): lax.all_to_all(fan_out(sent_x), 'own', split_axis=0, concat_axis=0, tiled...  61.1 us
    all_to_all x1, waiting for transfers between devices, per_device(): lax.all_to_all(fan_out(sent_cot), 'own', split_axis=0, concat_axis=0, til...  58.6 us
    all_to_all x1, starting transfers between devices, per_device(): lax.all_to_all(fan_out(sent_x), 'own', split_axis=0, concat_axis=0, tiled...  20.7 us
    all_to_all x1, starting transfers between devices, per_device(): lax.all_to_all(block_rows, 'own', split_axis=0, concat_axis=0, tiled=True)  19 us
    all_to_all x1, starting transfers between devices, per_device(): lax.all_to_all(fan_out(sent_cot), 'own', split_axis=0, concat_axis=0, til...  16.6 us
    eq x4, local copies, waits for them, and re-layouts, per_device(): earlier[:, :, None] == jnp.arange(CAP, dtype=jnp.int32)[None, None, :]  8.34 us
    mul x2, local copies, waits for them, and re-layouts, per_device(): is_named[:, :, None]  8.27 us
  transfers between devices with their start and end apart: 7, of which 3 were waited for; matrix products, arithmetic and copies ran while one was open for 7% of the time, Pallas kernels for 0%

commit v1 on v0

--- a/solution.py
+++ b/solution.py
@@ -29,47 +29,40 @@
     return (grad_rows, grad_gate, grad_up, grad_down)
 
 
+def slot_tables(route, gate_index, gate_table, experts_here):
+    tok_count, choices_each = route.shape
+    slots = experts_here * CAP
+    column = jnp.arange(slots, dtype=jnp.int32)[None, :]
+    pair_route = route.reshape(-1)[:, None]
+    is_named = (pair_route == column // CAP).astype(jnp.int32)
+    earlier = jnp.cumsum(is_named, axis=0) - is_named
+    hit = jnp.where(earlier == column % CAP, is_named, 0)
+    gate_values = jnp.take(gate_table, gate_index.reshape(-1), axis=0)
+    slot_gate = jnp.sum(jnp.where(hit > 0, gate_values[:, None], 0.0), axis=0)
+    select = hit.reshape(tok_count, choices_each, slots).sum(axis=1).astype(jnp.float32)
+    return select, slot_gate
+
+
 def per_device(tokens, cotangent, route, gate_index, gate_table, w_gate, w_up, w_down):
     owners = lax.axis_size("own")
     experts_here = owners // SPLIT
-    tok_count = tokens.shape[0]
     model_width = tokens.shape[1]
-    choices_each = route.shape[1]
-    table_hits = (
-        gate_index[:, :, None] == jnp.arange(gate_table.shape[0], dtype=jnp.int32)[None, None, :]
-    ).astype(jnp.float32)
-    gate_values = jnp.sum(table_hits * gate_table[None, None, :], axis=2).reshape(-1)
-    is_named = (
-        route.reshape(-1)[:, None] == jnp.arange(experts_here, dtype=jnp.int32)[None, :]
-    ).astype(jnp.int32)
-    earlier = jnp.cumsum(is_named, axis=0) - is_named
-    slot_hits = (
-        is_named[:, :, None]
-        * (earlier[:, :, None] == jnp.arange(CAP, dtype=jnp.int32)[None, None, :]).astype(jnp.int32)
-    ).astype(jnp.float32)
-    slot_hits = slot_hits.reshape(tok_count * choices_each, experts_here * CAP)
-    select = slot_hits.reshape(tok_count, choices_each, experts_here * CAP).sum(axis=1)
-    slot_gate = jnp.dot(
-        gate_values, slot_hits, precision=lax.Precision.HIGHEST, preferred_element_type=jnp.float32
-    )
+    select, slot_gate = slot_tables(route, gate_index, gate_table, experts_here)
     picker = select.astype(jnp.bfloat16)
     sent_x = jnp.dot(picker.T, tokens, preferred_element_type=jnp.float32).astype(jnp.bfloat16)
     sent_dy = jnp.dot(picker.T, cotangent, preferred_element_type=jnp.float32)
     sent_cot = (slot_gate[:, None] * sent_dy).astype(jnp.bfloat16)
 
-    def fan_out(slot_rows):
-        spread = jnp.broadcast_to(
-            slot_rows.reshape(experts_here, 1, CAP, model_width),
-            (experts_here, SPLIT, CAP, model_width),
-        )
-        return spread.reshape(owners, CAP, model_width)
-
-    got_x, got_cot = (
-        lax.all_to_all(fan_out(sent_x), "own", split_axis=0, concat_axis=0, tiled=True),
-        lax.all_to_all(fan_out(sent_cot), "own", split_axis=0, concat_axis=0, tiled=True),
+    both = jnp.concatenate(
+        [sent_x.reshape(experts_here, 1, CAP, model_width), sent_cot.reshape(experts_here, 1, CAP, model_width)],
+        axis=2,
     )
-    rows_x = got_x.reshape(owners * CAP, model_width)
-    rows_cot = got_cot.reshape(owners * CAP, model_width)
+    spread = jnp.broadcast_to(both, (experts_here, SPLIT, 2 * CAP, model_width)).reshape(
+        owners, 2 * CAP, model_width
+    )
+    got = lax.all_to_all(spread, "own", split_axis=0, concat_axis=0, tiled=True)
+    rows_x = got[:, :CAP].reshape(owners * CAP, model_width)
+    rows_cot = got[:, CAP:].reshape(owners * CAP, model_width)
     full_gate, full_up, full_down = (
         lax.all_gather(w_gate, "rep", axis=0, tiled=True),
         lax.all_gather(w_up, "rep", axis=0, tiled=True),
@@ -89,10 +82,8 @@
     grad_tokens = jnp.dot(
         select, per_slot, precision=lax.Precision.HIGHEST, preferred_element_type=jnp.float32
     ).astype(jnp.bfloat16)
-    stacked = jnp.stack([grad_gate, grad_up, grad_down]).astype(jnp.bfloat16).astype(jnp.float32)
-    totals_all = lax.psum(stacked.astype(jnp.bfloat16), "rep").astype(jnp.float32)
-    rows_each = stacked.shape[1] // lax.axis_size("rep")
-    shares = lax.dynamic_slice_in_dim(totals_all, lax.axis_index("rep") * rows_each, rows_each, 1)
+    stacked = jnp.stack([grad_gate, grad_up, grad_down]).astype(jnp.bfloat16)
+    shares = lax.psum_scatter(stacked, "rep", scatter_dimension=1, tiled=True).astype(jnp.float32)
     return (grad_tokens, shares[0], shares[1], shares[2])
 
 

time: 347 us -> 336 us (0.968)
  blocking collectives: 0 us -> 110 us
  waiting for transfers between devices: 203 us -> 140 us
  starting transfers between devices: 56.6 us -> 17 us
  other arithmetic: 14.3 us -> 6.6 us
  local copies, waits for them, and re-layouts: 36.9 us -> 31.4 us
    all_to_all x0 -> x1, blocking collectives: none -> 110 us  [per_device(): lax.all_to_all(block_rows, 'own', split_axis=0, concat_axis=0, tiled=True)]
    psum x1 -> x0, waiting for transfers between devices: 81.6 us -> none  [per_device(): lax.psum(stacked.astype(jnp.bfloat16), 'rep').astype(jnp.float32)]
    all_to_all x3 -> x1, starting transfers between devices: 56.3 us -> 16.8 us  [per_device(): got = lax.all_to_all(spread, 'own', split_axis=0, concat_axis=0, tiled=True)]
    all_to_all x3 -> x1, waiting for transfers between devices: 120 us -> 138 us  [per_device(): got = lax.all_to_all(spread, 'own', split_axis=0, concat_axis=0, tiled=True)]
    eq x6 -> x2, local copies, waits for them, and re-layouts: 8.6 us -> 0.26 us  [slot_tables(): is_named = (pair_route == column // CAP).astype(jnp.int32)]
    mul x2 -> x0, local copies, waits for them, and re-layouts: 8.27 us -> none  [per_device(): is_named[:, :, None]]
    slice x1 -> x2, local copies, waits for them, and re-layouts: 0.25 us -> 6.64 us  [the longest x1 6.35 us: per_device(): rows_cot = got[:, CAP:].reshape(owners * CAP, model_width)]
    reduce_sum x2, other arithmetic: 6.77 us -> 0.42 us  [the longest x1 0.26 us: slot_tables(): slot_gate = jnp.sum(jnp.where(hit > 0, gate_values[:, None], 0.0), axis=0)]
  transfers between devices with their start and end apart: 7 -> 5, of which waited for: 3 -> 1; matrix products, arithmetic and copies ran while one was open for 7% -> 8% of each run, Pallas kernels for 0% -> 0%
where the time goes in v1:
time: 336 us
  waiting for transfers between devices  140 us (42%)
  blocking collectives  110 us (33%)
  local copies, waits for them, and re-layouts  31.4 us (9%)
  starting transfers between devices  17 us (5%)
  matrix products  16.1 us (5%)
  between operations  14.1 us (4%)
  other arithmetic  6.6 us (2%)
    all_to_all x1, waiting for transfers between devices, per_device(): got = lax.all_to_all(spread, 'own', split_axis=0, concat_axis=0, tiled=True)  138 us
    all_to_all x1, blocking collectives, per_device(): lax.all_to_all(block_rows, 'own', split_axis=0, concat_axis=0, tiled=True)  110 us
    all_to_all x1, starting transfers between devices, per_device(): got = lax.all_to_all(spread, 'own', split_axis=0, concat_axis=0, tiled=True)  16.8 us
  transfers between devices with their start and end apart: 5, of which 1 were waited for; matrix products, arithmetic and copies ran while one was open for 8% of the time, Pallas kernels for 0%

profile of v1, /device:TPU:6, one launch (start us, length us, event | category | flops | bytes accessed | tf_op | source)
XLA Modules:
  0.0 335.5 jit_solution(12327172025850917324)
XLA Ops:
  7.2 0.9 copy.16
  8.1 0.1 reshape.149
  8.2 0.1 reshape.148
  8.3 0.8 copy.12
  9.1 0.1 eq.35
  9.3 0.1 eq.39
  9.4 0.1 compare_convert_fusion
  9.5 1.9 reduce-window.6
  11.4 0.3 slice_reduce_fusion
  11.8 5.0 %gather_fusion = f32[768]{0:T(1024)S(1)} fusion(f32[256]{0:T(256)S(1)} %copy-done.1, s32[1024]{0:T(1024)S(1)} %pad_clamp_fusion), kind=kCustom, calls=%fused_computation | custom fusion | bytes 9216 | tf_op jit(solution)/shard_map/jit(_take)/gather | solution.py:40
  16.8 0.3 select_reduce_fusion
  17.0 0.2 copy.15
  17.3 0.2 reduce_sum.27
  17.5 0.3 fusion.4
  17.8 0.2 reshape.150
  18.0 0.3 copy-done.6
  18.3 0.3 convolution_convert_fusion.4
  18.6 0.2 reshape.147
  18.8 0.4 maximum_bitcast_fusion
  19.2 3.0 broadcast_in_dim.37
  22.2 16.8 %all-to-all-start = ((bf16[64,12,2560]{2,1,0:T(8,128)(2,1)}), bf16[64,12,2560]{2,1,0:T(8,128)(2,1)}, u32[]{:S(2)}, u32[]{:S(2)}) async-start(bf16[64,12,2560]{2,1,0:T(8,128)(2,1)} %bitcast.54), calls=%async_computation | async-start | bytes 10485760 | tf_op jit(solution)/shard_map/all_to_all | solution.py:63
  39.1 0.7 all-gather.6.cloned.1.call-update
  39.8 0.7 all-gather.8.cloned.1.call-update
  40.5 0.7 all-gather.4.cloned.1.call-update
  41.3 138.3 %all-to-all-done = bf16[64,12,2560]{2,1,0:T(8,128)(2,1)} async-done(((bf16[64,12,2560]{2,1,0:T(8,128)(2,1)}), bf16[64,12,2560]{2,1,0:T(8,128)(2,1)}, u32[]{:S(2)}, u32[]{:S(2)}) %all-to-all-start) | async-done | bytes 3932192 | tf_op jit(solution)/shard_map/all_to_all | solution.py:63
  179.6 6.4 %fusion.11 = (bf16[64,6,2560]{2,1,0:T(8,128)(2,1)}, bf16[64,6,2560]{2,1,0:T(8,128)(2,1)}) fusion(bf16[64,12,2560]{2,1,0:T(8,128)(2,1)} %all-to-all-done), kind=kLoop, calls=%fused_computation.45 | loop fusion | bytes 7864320 | tf_op jit(solution)/shard_map/slice | solution.py:65
  185.9 2.8 reshape.153
  188.7 4.1 %reshape.152 = bf16[384,2560]{1,0:T(8,128)(2,1)} reshape(bf16[64,6,2560]{2,1,0:T(8,128)(2,1)} %get-tuple-element.6) | data formatting | bytes 3932160 | tf_op jit(solution)/shard_map/reshape | solution.py:65
  192.8 2.0 fusion.12
  194.9 2.2 fusion.13
  197.1 0.7 copy-done.8
  197.8 2.0 fusion.3
  199.8 2.8 multiply_convert_fusion.1
  202.7 0.9 fusion.1
  203.5 0.9 fusion.2
  204.4 0.4 copy-done.3
  204.9 2.1 pad_maximum_fusion
  207.0 1.3 copy-done.5
  208.3 0.7 fusion.14
  208.9 0.6 copy-done.4
  209.6 2.0 fusion
  211.6 2.6 reshape.154
  214.2 110.0 %all_to_all.10 = bf16[64,6,2560]{2,1,0:T(8,128)(2,1)S(1)} all-to-all(bf16[64,6,2560]{2,1,0:T(8,128)(2,1)S(1)} %reshape.154), channel_id=1, replica_groups=mesh['own'=64,'rep'=8] {'own'}, dimensions={0} | all-to-all | bytes 3932160 | tf_op jit(solution)/shard_map/all_to_all | solution.py:75
  324.1 0.5 convert_reduce_fusion
  324.7 0.1 reshape.157
  324.8 2.1 convolution_convert_fusion.3
  326.9 1.1 convert_element_type.50
  328.0 1.0 slice_bitcast_fusion
  (28 shorter events, 0.3 us)
Async XLA Ops:
  7.2 10.3 %copy-start = (bf16[128,2560]{1,0:T(8,128)(2,1)S(1)}, bf16[128,2560]{1,0:T(8,128)(2,1)}, u32[]{:S(2)}) copy-start(bf16[128,2560]{1,0:T(8,128)(2,1)} %param.9) | copy-start | bytes 1966084
  7.2 4.6 %copy-start.1 = (f32[256]{0:T(256)S(1)}, f32[256]{0:T(256)}, u32[]{:S(2)}) copy-start(f32[256]{0:T(256)} %param.12) | copy-start | bytes 3076
  17.2 1.1 copy-start.6
  22.2 157.4 %all-to-all-start = ((bf16[64,12,2560]{2,1,0:T(8,128)(2,1)}), bf16[64,12,2560]{2,1,0:T(8,128)(2,1)}, u32[]{:S(2)}, u32[]{:S(2)}) async-start(bf16[64,12,2560]{2,1,0:T(8,128)(2,1)} %bitcast.54), calls=%async_computation | async-start | bytes 10485760 | tf_op jit(solution)/shard_map/all_to_all | solution.py:63
  39.0 153.8 %all-gather.6.cloned.1.call-start = ((), (), s32[]{:S(2)}) async-start(), calls=%async_computation.4 | async-start | bytes 1474560 | tf_op jit(solution)/shard_map/all_gather | solution.py:68
  39.8 155.1 %all-gather.8.cloned.1.call-start = ((), (), s32[]{:S(2)}) async-start(), calls=%async_computation.5 | async-start | bytes 1474560 | tf_op jit(solution)/shard_map/all_gather | solution.py:67
  40.5 159.3 %all-gather.4.cloned.1.call-start = ((), (), s32[]{:S(2)}) async-start(), calls=%async_computation.3 | async-start | bytes 1474560 | tf_op jit(solution)/shard_map/all_gather | solution.py:69
  41.2 285.7 %reduce-scatter.2.cloned.1.call-start = ((), (), s32[]{:S(2)}) async-start(), calls=%async_computation.6 | async-start | bytes 4423680 | tf_op jit(solution)/shard_map/reduce_scatter | solution.py:86
  194.8 2.2 copy-start.7
  194.9 3.0 copy-start.2
  197.1 0.7 copy-start.8
  203.5 1.3 copy-start.3
  206.9 1.3 copy-start.5
  208.2 1.3 copy-start.4
Sparse Core Ops, SparseCore 0:
  41.9 28.2 all-gather.5
  72.4 29.0 all-gather.7
  103.6 29.0 all-gather.3
  207.1 72.8 reduce-scatter.1

commit v2 on v1

--- a/solution.py
+++ b/solution.py
@@ -58,9 +58,10 @@
         axis=2,
     )
     spread = jnp.broadcast_to(both, (experts_here, SPLIT, 2 * CAP, model_width)).reshape(
-        owners, 2 * CAP, model_width
+        owners, 16, -1
     )
     got = lax.all_to_all(spread, "own", split_axis=0, concat_axis=0, tiled=True)
+    got = got.reshape(owners, 2 * CAP, model_width)
     rows_x = got[:, :CAP].reshape(owners * CAP, model_width)
     rows_cot = got[:, CAP:].reshape(owners * CAP, model_width)
     full_gate, full_up, full_down = (
@@ -71,10 +72,10 @@
     grad_rows, grad_gate, grad_up, grad_down = panel_terms(
         rows_x, rows_cot, full_gate, full_up, full_down
     )
-    block_rows = grad_rows.astype(jnp.bfloat16).reshape(owners, CAP, model_width)
+    block_rows = grad_rows.astype(jnp.bfloat16).reshape(owners, 16, -1)
     returned = lax.all_to_all(block_rows, "own", split_axis=0, concat_axis=0, tiled=True)
     per_slot = (
-        returned.astype(jnp.float32)
+        returned.reshape(owners, CAP, model_width).astype(jnp.float32)
         .reshape(experts_here, SPLIT, CAP, model_width)
         .sum(axis=1)
         .reshape(experts_here * CAP, model_width)

time: 336 us -> 291 us (0.87)
  waiting for transfers between devices: 140 us -> 96 us
  blocking collectives: 110 us -> 84.3 us
  local copies, waits for them, and re-layouts: 31.4 us -> 53.2 us
    all_to_all x1, waiting for transfers between devices: 138 us -> 93.9 us  [per_device(): got = lax.all_to_all(spread, 'own', split_axis=0, concat_axis=0, tiled=True)]
    all_to_all x1, blocking collectives: 110 us -> 84.3 us  [per_device(): lax.all_to_all(block_rows, 'own', split_axis=0, concat_axis=0, tiled=True)]
    reshape x2 -> x4, local copies, waits for them, and re-layouts: 2.76 us -> 20.6 us  [the longest x1 8.06 us: per_device(): jnp.broadcast_to(both, (experts_here, SPLIT, 2 * CAP, model_width))]
    convert_element_type x0 -> x1, local copies, waits for them, and re-layouts: none -> 4.62 us  [per_device(): returned.reshape(owners, CAP, model_width).astype(jnp.float32)]
  transfers between devices with their start and end apart: 5 -> 5, of which waited for: 1 -> 1; matrix products, arithmetic and copies ran while one was open for 8% -> 15% of each run, Pallas kernels for 0% -> 0%
where the time goes in v2:
time: 291 us; the launch traced here: 289 us
  waiting for transfers between devices  96 us (33%)
  blocking collectives  84.3 us (29%)
  local copies, waits for them, and re-layouts  53.2 us (18%)
  starting transfers between devices  17.1 us (6%)
  matrix products  14.6 us (5%)
  between operations  14.1 us (5%)
  other arithmetic  9.39 us (3%)
    all_to_all x1, waiting for transfers between devices, per_device(): got = lax.all_to_all(spread, 'own', split_axis=0, concat_axis=0, tiled=True)  93.9 us
    all_to_all x1, blocking collectives, per_device(): lax.all_to_all(block_rows, 'own', split_axis=0, concat_axis=0, tiled=True)  84.3 us
    all_to_all x1, starting transfers between devices, per_device(): got = lax.all_to_all(spread, 'own', split_axis=0, concat_axis=0, tiled=True)  16.8 us
    reshape x1, local copies, waits for them, and re-layouts, per_device(): jnp.broadcast_to(both, (experts_here, SPLIT, 2 * CAP, model_width))  8.06 us
    reshape x1, local copies, waits for them, and re-layouts, per_device(): got = got.reshape(owners, 2 * CAP, model_width)  8.04 us
    slice x1, local copies, waits for them, and re-layouts, per_device(): rows_cot = got[:, CAP:].reshape(owners * CAP, model_width)  6.34 us
  transfers between devices with their start and end apart: 5, of which 1 were waited for; matrix products, arithmetic and copies ran while one was open for 15% of the time, Pallas kernels for 0%

profile of v2, /device:TPU:6, one launch (start us, length us, event | category | flops | bytes accessed | tf_op | source)
XLA Modules:
  0.0 288.7 jit_solution(8500949968363122285)
XLA Ops:
  7.2 0.9 copy.16
  8.1 0.1 reshape.151
  8.2 0.1 reshape.150
  8.3 0.8 copy.12
  9.5 1.9 reduce-window.6
  11.4 0.3 slice_reduce_fusion
  11.8 5.0 %gather_fusion = f32[768]{0:T(1024)S(1)} fusion(f32[256]{0:T(256)S(1)} %copy-done.2, s32[1024]{0:T(1024)S(1)} %pad_clamp_fusion), kind=kCustom, calls=%fused_computation | custom fusion | bytes 9216 | tf_op jit(solution)/shard_map/jit(_take)/gather | solution.py:40
  16.8 0.3 select_reduce_fusion
  17.0 0.2 copy.15
  17.3 0.2 reduce_sum.27
  17.5 0.3 fusion.4
  17.8 0.2 reshape.152
  18.0 0.3 copy-done.7
  18.3 0.3 convolution_convert_fusion.4
  18.6 0.2 reshape.149
  18.8 0.4 maximum_bitcast_fusion
  19.2 2.9 %broadcast_in_dim.37 = bf16[16,4,12,2560]{3,2,1,0:T(8,128)(2,1)} broadcast(bf16[16,12,2560]{2,1,0:T(8,128)(2,1)S(1)} %maximum_bitcast_fusion), dimensions={0,2,3} | broadcast | bytes 4915200 | tf_op jit(solution)/shard_map/broadcast_in_dim | solution.py:60
  22.2 8.1 %reshape.153 = bf16[64,16,1920]{2,1,0:T(8,128)(2,1)} reshape(bf16[16,4,12,2560]{3,2,1,0:T(8,128)(2,1)} %broadcast_in_dim.37) | data formatting | bytes 7864320 | tf_op jit(solution)/shard_map/reshape | solution.py:60
  30.2 16.8 %all-to-all-start = ((bf16[64,16,1920]{2,1,0:T(8,128)(2,1)}), bf16[64,16,1920]{2,1,0:T(8,128)(2,1)}, u32[]{:S(2)}, u32[]{:S(2)}) async-start(bf16[64,16,1920]{2,1,0:T(8,128)(2,1)} %reshape.153), calls=%async_computation | async-start | bytes 7864320 | tf_op jit(solution)/shard_map/all_to_all | solution.py:63
  47.1 0.7 all-gather.6.cloned.1.call-update
  47.8 0.7 all-gather.8.cloned.1.call-update
  48.6 0.7 all-gather.4.cloned.1.call-update
  49.3 0.2 reduce-scatter.2.cloned.1.call-start
  49.5 93.9 %all-to-all-done = bf16[64,16,1920]{2,1,0:T(8,128)(2,1)} async-done(((bf16[64,16,1920]{2,1,0:T(8,128)(2,1)}), bf16[64,16,1920]{2,1,0:T(8,128)(2,1)}, u32[]{:S(2)}, u32[]{:S(2)}) %all-to-all-start) | async-done | bytes 3932192 | tf_op jit(solution)/shard_map/all_to_all | solution.py:63
  143.4 8.0 %reshape.154 = bf16[64,12,2560]{2,1,0:T(8,128)(2,1)} reshape(bf16[64,16,1920]{2,1,0:T(8,128)(2,1)} %all-to-all-done) | data formatting | bytes 7864320 | tf_op jit(solution)/shard_map/reshape | solution.py:64
  151.4 6.3 %fusion.11 = (bf16[64,6,2560]{2,1,0:T(8,128)(2,1)}, bf16[64,6,2560]{2,1,0:T(8,128)(2,1)}) fusion(bf16[64,12,2560]{2,1,0:T(8,128)(2,1)} %reshape.154), kind=kLoop, calls=%fused_computation.44 | loop fusion | bytes 7864320 | tf_op jit(solution)/shard_map/slice | solution.py:66
  157.8 2.8 reshape.156
  160.5 4.2 %reshape.155 = bf16[384,2560]{1,0:T(8,128)(2,1)} reshape(bf16[64,6,2560]{2,1,0:T(8,128)(2,1)} %get-tuple-element.6) | data formatting | bytes 3932160 | tf_op jit(solution)/shard_map/reshape | solution.py:66
  164.7 2.0 fusion.12
  166.8 2.2 fusion.13
  169.0 2.0 fusion.3
  171.0 2.6 multiply_convert_fusion.1
  173.6 0.9 fusion.1
  174.5 0.9 fusion.2
  175.4 0.4 copy-done.4
  175.8 2.2 pad_maximum_fusion
  178.0 1.3 copy-done.6
  179.3 0.7 fusion.14
  180.0 0.6 copy-done.5
  180.6 0.7 fusion
  181.3 4.4 %reshape.157 = bf16[64,16,960]{2,1,0:T(8,128)(2,1)} reshape(bf16[384,2560]{1,0:T(8,128)(2,1)S(1)} %fusion) | data formatting | bytes 3932160 | tf_op jit(solution)/shard_map/reshape | solution.py:75
  185.7 84.3 %all_to_all.10 = bf16[64,16,960]{2,1,0:T(8,128)(2,1)S(1)} all-to-all(bf16[64,16,960]{2,1,0:T(8,128)(2,1)} %reshape.157), channel_id=1, replica_groups=mesh['own'=64,'rep'=8] {'own'}, dimensions={0} | all-to-all | bytes 3932160 | tf_op jit(solution)/shard_map/all_to_all | solution.py:76
  270.0 4.6 %reshape.159 = f32[16,4,6,2560]{3,2,1,0:T(8,128)} reshape(bf16[64,16,960]{2,1,0:T(8,128)(2,1)S(1)} %all_to_all.10) | data formatting | bytes 5898240 | tf_op jit(solution)/shard_map/convert_element_type | solution.py:78
  274.6 3.2 %reduce_sum.29 = f32[16,6,2560]{2,1,0:T(8,128)S(1)} reduce(f32[16,4,6,2560]{3,2,1,0:T(8,128)} %reshape.159, f32[]{:T(128)} %constant.42.clone.1), dimensions={1}, to_apply=%region_4.5 | reduce | flops 737280 | bytes 4915204 | tf_op jit(solution)/shard_map/reduce_sum | solution.py:80
  277.9 0.1 reshape.158
  278.0 2.1 convolution_convert_fusion.3
  280.1 1.1 convert_element_type.58
  281.2 1.0 slice_bitcast_fusion
  (29 shorter events, 0.7 us)
Async XLA Ops:
  7.2 10.3 %copy-start = (bf16[128,2560]{1,0:T(8,128)(2,1)S(1)}, bf16[128,2560]{1,0:T(8,128)(2,1)}, u32[]{:S(2)}) copy-start(bf16[128,2560]{1,0:T(8,128)(2,1)} %param.9) | copy-start | bytes 1966084
  7.2 4.6 %copy-start.2 = (f32[256]{0:T(256)S(1)}, f32[256]{0:T(256)}, u32[]{:S(2)}) copy-start(f32[256]{0:T(256)} %param.12) | copy-start | bytes 3076
  17.2 1.1 copy-start.7
  30.2 113.2 %all-to-all-start = ((bf16[64,16,1920]{2,1,0:T(8,128)(2,1)}), bf16[64,16,1920]{2,1,0:T(8,128)(2,1)}, u32[]{:S(2)}, u32[]{:S(2)}) async-start(bf16[64,16,1920]{2,1,0:T(8,128)(2,1)} %reshape.153), calls=%async_computation | async-start | bytes 7864320 | tf_op jit(solution)/shard_map/all_to_all | solution.py:63
  47.0 117.7 %all-gather.6.cloned.1.call-start = ((), (), s32[]{:S(2)}) async-start(), calls=%async_computation.4 | async-start | bytes 1474560 | tf_op jit(solution)/shard_map/all_gather | solution.py:69
  47.8 119.0 %all-gather.8.cloned.1.call-start = ((), (), s32[]{:S(2)}) async-start(), calls=%async_computation.5 | async-start | bytes 1474560 | tf_op jit(solution)/shard_map/all_gather | solution.py:68
  48.5 122.4 %all-gather.4.cloned.1.call-start = ((), (), s32[]{:S(2)}) async-start(), calls=%async_computation.3 | async-start | bytes 1474560 | tf_op jit(solution)/shard_map/all_gather | solution.py:70
  49.3 230.8 %reduce-scatter.2.cloned.1.call-start = ((), (), s32[]{:S(2)}) async-start(), calls=%async_computation.6 | async-start | bytes 4423680 | tf_op jit(solution)/shard_map/reduce_scatter | solution.py:87
  166.8 2.2 copy-start.3
  174.5 1.3 copy-start.4
  178.0 1.3 copy-start.6
  179.3 1.3 copy-start.5
  278.0 4.2 %copy-start.1 = (bf16[128,2560]{1,0:T(8,128)(2,1)S(1)}, bf16[128,2560]{1,0:T(8,128)(2,1)}, u32[]{:S(2)}) copy-start(bf16[128,2560]{1,0:T(8,128)(2,1)} %param.9) | copy-start | bytes 1966084
Sparse Core Ops, SparseCore 0:
  50.0 28.3 all-gather.5
  80.4 29.0 all-gather.7
  111.7 29.0 all-gather.3
  178.1 60.5 reduce-scatter.1

commit v3 on v2

--- a/solution.py
+++ b/solution.py
@@ -54,16 +54,13 @@
     sent_cot = (slot_gate[:, None] * sent_dy).astype(jnp.bfloat16)
 
     both = jnp.concatenate(
-        [sent_x.reshape(experts_here, 1, CAP, model_width), sent_cot.reshape(experts_here, 1, CAP, model_width)],
-        axis=2,
-    )
-    spread = jnp.broadcast_to(both, (experts_here, SPLIT, 2 * CAP, model_width)).reshape(
-        owners, 16, -1
-    )
+        [sent_x.reshape(experts_here, CAP, model_width), sent_cot.reshape(experts_here, CAP, model_width)],
+        axis=1,
+    ).reshape(experts_here, 1, 16, -1)
+    spread = jnp.broadcast_to(both, (experts_here, SPLIT) + both.shape[2:]).reshape(owners, 16, -1)
     got = lax.all_to_all(spread, "own", split_axis=0, concat_axis=0, tiled=True)
-    got = got.reshape(owners, 2 * CAP, model_width)
-    rows_x = got[:, :CAP].reshape(owners * CAP, model_width)
-    rows_cot = got[:, CAP:].reshape(owners * CAP, model_width)
+    rows_x = got[:, :8].reshape(owners * CAP, model_width)
+    rows_cot = got[:, 8:].reshape(owners * CAP, model_width)
     full_gate, full_up, full_down = (
         lax.all_gather(w_gate, "rep", axis=0, tiled=True),
         lax.all_gather(w_up, "rep", axis=0, tiled=True),
@@ -75,8 +72,8 @@
     block_rows = grad_rows.astype(jnp.bfloat16).reshape(owners, 16, -1)
     returned = lax.all_to_all(block_rows, "own", split_axis=0, concat_axis=0, tiled=True)
     per_slot = (
-        returned.reshape(owners, CAP, model_width).astype(jnp.float32)
-        .reshape(experts_here, SPLIT, CAP, model_width)
+        returned.reshape(experts_here, SPLIT, 16, returned.shape[-1])
+        .astype(jnp.float32)
         .sum(axis=1)
         .reshape(experts_here * CAP, model_width)
     )

time: 291 us -> 269 us (0.924)
  local copies, waits for them, and re-layouts: 53.2 us -> 32.8 us
  other arithmetic: 9.39 us -> 6.47 us
    reshape x7 -> x5, local copies, waits for them, and re-layouts: 23.5 us -> 8.68 us  [the longest x1 4.33 us: per_device(): rows_cot = got[:, 8:].reshape(owners * CAP, model_width)]
    convert_element_type x1 -> x0, local copies, waits for them, and re-layouts: 4.62 us -> none  [per_device(): returned.reshape(owners, CAP, model_width).astype(jnp.float32)]
  transfers between devices with their start and end apart: 5 -> 5, of which waited for: 1 -> 1; matrix products, arithmetic and copies ran while one was open for 15% -> 11% of each run, Pallas kernels for 0% -> 0%
where the time goes in v3:
time: 269 us; the launch traced here: 265 us
  waiting for transfers between devices  96 us (36%)
  blocking collectives  82.2 us (31%)
  local copies, waits for them, and re-layouts  32.8 us (12%)
  starting transfers between devices  17.2 us (6%)
  matrix products  16.1 us (6%)
  between operations  14.1 us (5%)
  other arithmetic  6.47 us (2%)
    all_to_all x1, waiting for transfers between devices, per_device(): got = lax.all_to_all(spread, 'own', split_axis=0, concat_axis=0, tiled=True)  93.9 us
    all_to_all x1, blocking collectives, per_device(): lax.all_to_all(block_rows, 'own', split_axis=0, concat_axis=0, tiled=True)  82.2 us
    all_to_all x1, starting transfers between devices, per_device(): got = lax.all_to_all(spread, 'own', split_axis=0, concat_axis=0, tiled=True)  16.8 us
  transfers between devices with their start and end apart: 5, of which 1 were waited for; matrix products, arithmetic and copies ran while one was open for 11% of the time, Pallas kernels for 0%

profile of v3, /device:TPU:6, one launch (start us, length us, event | category | flops | bytes accessed | tf_op | source)
XLA Modules:
  0.0 264.7 jit_solution(17507594189273354289)
XLA Ops:
  7.2 0.9 copy.16
  8.1 0.1 reshape.148
  8.2 0.1 reshape.147
  8.3 0.8 copy.12
  9.1 0.1 eq.35
  9.5 1.9 reduce-window.6
  11.4 0.3 slice_reduce_fusion
  11.8 5.0 %gather_fusion = f32[768]{0:T(1024)S(1)} fusion(f32[256]{0:T(256)S(1)} %copy-done.1, s32[1024]{0:T(1024)S(1)} %pad_clamp_fusion), kind=kCustom, calls=%fused_computation | custom fusion | bytes 9216 | tf_op jit(solution)/shard_map/jit(_take)/gather | solution.py:40
  16.8 0.3 select_reduce_fusion
  17.0 0.2 copy.15
  17.3 0.2 reduce_sum.27
  17.5 0.3 fusion.4
  17.8 0.2 reshape.149
  18.0 0.3 copy-done.6
  18.3 0.3 convolution_convert_fusion.4
  18.6 0.2 reshape.146
  18.8 0.4 pad_maximum_fusion.1
  19.2 0.8 broadcast_in_dim.36
  20.1 2.2 broadcast_in_dim.37
  22.2 16.8 %all-to-all-start = ((bf16[64,16,1920]{2,1,0:T(8,128)(2,1)}), bf16[64,16,1920]{2,1,0:T(8,128)(2,1)}, u32[]{:S(2)}, u32[]{:S(2)}) async-start(bf16[64,16,1920]{2,1,0:T(8,128)(2,1)} %bitcast.52), calls=%async_computation | async-start | bytes 7864320 | tf_op jit(solution)/shard_map/all_to_all | solution.py:61
  39.1 0.7 all-gather.6.cloned.1.call-update
  39.8 0.7 all-gather.8.cloned.1.call-update
  40.6 0.7 all-gather.4.cloned.1.call-update
  41.3 0.2 reduce-scatter.2.cloned.1.call-start
  41.5 93.9 %all-to-all-done = bf16[64,16,1920]{2,1,0:T(8,128)(2,1)} async-done(((bf16[64,16,1920]{2,1,0:T(8,128)(2,1)}), bf16[64,16,1920]{2,1,0:T(8,128)(2,1)}, u32[]{:S(2)}, u32[]{:S(2)}) %all-to-all-start) | async-done | bytes 3932192 | tf_op jit(solution)/shard_map/all_to_all | solution.py:61
  135.4 4.3 %fusion.11 = (bf16[64,8,1920]{2,1,0:T(8,128)(2,1)}, bf16[64,8,1920]{2,1,0:T(8,128)(2,1)}) fusion(bf16[64,16,1920]{2,1,0:T(8,128)(2,1)} %all-to-all-done), kind=kLoop, calls=%fused_computation.45 | loop fusion | bytes 7864320 | tf_op jit(solution)/shard_map/slice | solution.py:63
  139.7 3.3 %reshape.152 = bf16[384,2560]{1,0:T(8,128)(2,1)S(1)} reshape(bf16[64,8,1920]{2,1,0:T(8,128)(2,1)} %get-tuple-element.7) | data formatting | bytes 3932160 | tf_op jit(solution)/shard_map/reshape | solution.py:62
  143.1 4.3 %reshape.151 = bf16[384,2560]{1,0:T(8,128)(2,1)} reshape(bf16[64,8,1920]{2,1,0:T(8,128)(2,1)} %get-tuple-element.6) | data formatting | bytes 3932160 | tf_op jit(solution)/shard_map/reshape | solution.py:63
  147.4 2.0 fusion.12
  149.5 2.2 fusion.13
  151.7 0.7 copy-done.8
  152.4 2.0 fusion.3
  154.4 2.8 %multiply_convert_fusion.1 = (bf16[384,256]{1,0:T(8,128)(2,1)S(1)}, bf16[384,256]{1,0:T(8,128)(2,1)S(1)}) fusion(f32[384,256]{1,0:T(8,128)} %copy-done.8, f32[384,256]{1,0:T(8,128)} %copy-done.7, bf16[384,2560]{1,0:T(8,128)(2,1)} %reshape.151, bf16[256,2560]{1,0:T(8,128)(2,1)} %all-gather.4.cloned.1.call-done), kind=kOutput, calls=%fused_computation.19 | convolution fusion | flops 504594432 | bytes 4456448 | tf_op jit(solution)/shard_map/dot_general | solution.py:20
  157.3 0.9 fusion.1
  158.1 0.9 fusion.2
  159.0 0.4 copy-done.3
  159.4 2.1 pad_maximum_fusion
  161.5 1.3 copy-done.5
  162.8 0.7 fusion.14
  163.5 0.6 copy-done.4
  164.2 2.0 fusion
  166.2 4.6 %reshape.153 = bf16[64,16,960]{2,1,0:T(8,128)(2,1)S(1)} reshape(bf16[384,2560]{1,0:T(8,128)(2,1)} %fusion) | data formatting | bytes 3932160 | tf_op jit(solution)/shard_map/reshape | solution.py:72
  170.8 82.2 %all_to_all.10 = bf16[64,16,960]{2,1,0:T(8,128)(2,1)S(1)} all-to-all(bf16[64,16,960]{2,1,0:T(8,128)(2,1)S(1)} %reshape.153), channel_id=1, replica_groups=mesh['own'=64,'rep'=8] {'own'}, dimensions={0} | all-to-all | bytes 3932160 | tf_op jit(solution)/shard_map/all_to_all | solution.py:73
  253.0 0.4 convert_reduce_fusion
  253.4 0.7 reshape.154
  254.1 2.1 convolution_convert_fusion.3
  256.1 1.1 convert_element_type.57
  257.3 1.0 slice_bitcast_fusion
  (29 shorter events, 0.5 us)
Async XLA Ops:
  7.2 10.3 %copy-start = (bf16[128,2560]{1,0:T(8,128)(2,1)S(1)}, bf16[128,2560]{1,0:T(8,128)(2,1)}, u32[]{:S(2)}) copy-start(bf16[128,2560]{1,0:T(8,128)(2,1)} %param.9) | copy-start | bytes 1966084
  7.2 4.6 %copy-start.1 = (f32[256]{0:T(256)S(1)}, f32[256]{0:T(256)}, u32[]{:S(2)}) copy-start(f32[256]{0:T(256)} %param.12) | copy-start | bytes 3076
  17.2 1.1 copy-start.6
  22.2 113.2 %all-to-all-start = ((bf16[64,16,1920]{2,1,0:T(8,128)(2,1)}), bf16[64,16,1920]{2,1,0:T(8,128)(2,1)}, u32[]{:S(2)}, u32[]{:S(2)}) async-start(bf16[64,16,1920]{2,1,0:T(8,128)(2,1)} %bitcast.52), calls=%async_computation | async-start | bytes 7864320 | tf_op jit(solution)/shard_map/all_to_all | solution.py:61
  39.1 108.4 %all-gather.6.cloned.1.call-start = ((), (), s32[]{:S(2)}) async-start(), calls=%async_computation.4 | async-start | bytes 1474560 | tf_op jit(solution)/shard_map/all_gather | solution.py:66
  39.8 109.7 %all-gather.8.cloned.1.call-start = ((), (), s32[]{:S(2)}) async-start(), calls=%async_computation.5 | async-start | bytes 1474560 | tf_op jit(solution)/shard_map/all_gather | solution.py:65
  40.6 113.9 %all-gather.4.cloned.1.call-start = ((), (), s32[]{:S(2)}) async-start(), calls=%async_computation.3 | async-start | bytes 1474560 | tf_op jit(solution)/shard_map/all_gather | solution.py:67
  41.3 214.8 %reduce-scatter.2.cloned.1.call-start = ((), (), s32[]{:S(2)}) async-start(), calls=%async_computation.6 | async-start | bytes 4423680 | tf_op jit(solution)/shard_map/reduce_scatter | solution.py:84
  149.4 2.2 copy-start.7
  149.5 3.0 %copy-start.2 = (bf16[384,2560]{1,0:T(8,128)(2,1)S(1)}, bf16[384,2560]{1,0:T(8,128)(2,1)}, u32[]{:S(2)}) copy-start(bf16[384,2560]{1,0:T(8,128)(2,1)} %reshape.151) | copy-start | bytes 5898244
  151.7 0.7 copy-start.8
  158.1 1.3 copy-start.3
  161.5 1.3 copy-start.5
  162.8 1.3 copy-start.4
Sparse Core Ops, SparseCore 0:
  42.0 28.3 all-gather.5
  72.5 29.0 all-gather.7
  103.7 29.0 all-gather.3
  161.7 62.4 reduce-scatter.1

commit v4 on v3

--- a/solution.py
+++ b/solution.py
@@ -53,34 +53,45 @@
     sent_dy = jnp.dot(picker.T, cotangent, preferred_element_type=jnp.float32)
     sent_cot = (slot_gate[:, None] * sent_dy).astype(jnp.bfloat16)
 
-    both = jnp.concatenate(
-        [sent_x.reshape(experts_here, CAP, model_width), sent_cot.reshape(experts_here, CAP, model_width)],
-        axis=1,
-    ).reshape(experts_here, 1, 16, -1)
-    spread = jnp.broadcast_to(both, (experts_here, SPLIT) + both.shape[2:]).reshape(owners, 16, -1)
-    got = lax.all_to_all(spread, "own", split_axis=0, concat_axis=0, tiled=True)
-    rows_x = got[:, :8].reshape(owners * CAP, model_width)
-    rows_cot = got[:, 8:].reshape(owners * CAP, model_width)
     full_gate, full_up, full_down = (
         lax.all_gather(w_gate, "rep", axis=0, tiled=True),
         lax.all_gather(w_up, "rep", axis=0, tiled=True),
         lax.all_gather(w_down, "rep", axis=0, tiled=True),
     )
-    grad_rows, grad_gate, grad_up, grad_down = panel_terms(
-        rows_x, rows_cot, full_gate, full_up, full_down
-    )
-    block_rows = grad_rows.astype(jnp.bfloat16).reshape(owners, 16, -1)
-    returned = lax.all_to_all(block_rows, "own", split_axis=0, concat_axis=0, tiled=True)
-    per_slot = (
-        returned.reshape(experts_here, SPLIT, 16, returned.shape[-1])
-        .astype(jnp.float32)
-        .sum(axis=1)
-        .reshape(experts_here * CAP, model_width)
-    )
+    x_slots = sent_x.reshape(experts_here, CAP, model_width)
+    cot_slots = sent_cot.reshape(experts_here, CAP, model_width)
+    chunk = CAP // 2
+    received = []
+    for part in range(2):
+        cut = slice(part * chunk, (part + 1) * chunk)
+        both = jnp.concatenate([x_slots[:, cut], cot_slots[:, cut]], axis=1).reshape(
+            experts_here, 1, 16, -1
+        )
+        spread = jnp.broadcast_to(both, (experts_here, SPLIT) + both.shape[2:]).reshape(owners, 16, -1)
+        received.append(lax.all_to_all(spread, "own", split_axis=0, concat_axis=0, tiled=True))
+    weight_sums = None
+    slot_parts = []
+    for got in received:
+        rows_x = got[:, :8].reshape(owners * chunk, model_width)
+        rows_cot = got[:, 8:].reshape(owners * chunk, model_width)
+        grad_rows, grad_gate, grad_up, grad_down = panel_terms(
+            rows_x, rows_cot, full_gate, full_up, full_down
+        )
+        terms = (grad_gate, grad_up, grad_down)
+        weight_sums = terms if weight_sums is None else tuple(a + b for a, b in zip(weight_sums, terms))
+        block_rows = grad_rows.astype(jnp.bfloat16).reshape(owners, 16, -1)
+        returned = lax.all_to_all(block_rows, "own", split_axis=0, concat_axis=0, tiled=True)
+        slot_parts.append(
+            returned.reshape(experts_here, SPLIT, 16, returned.shape[-1])
+            .astype(jnp.float32)
+            .sum(axis=1)
+            .reshape(experts_here, chunk, model_width)
+        )
+    per_slot = jnp.concatenate(slot_parts, axis=1).reshape(experts_here * CAP, model_width)
     grad_tokens = jnp.dot(
         select, per_slot, precision=lax.Precision.HIGHEST, preferred_element_type=jnp.float32
     ).astype(jnp.bfloat16)
-    stacked = jnp.stack([grad_gate, grad_up, grad_down]).astype(jnp.bfloat16)
+    stacked = jnp.stack(weight_sums).astype(jnp.bfloat16)
     shares = lax.psum_scatter(stacked, "rep", scatter_dimension=1, tiled=True).astype(jnp.float32)
     return (grad_tokens, shares[0], shares[1], shares[2])
 

time: 269 us -> 281 us (1.045)
  blocking collectives: 82.2 us -> 0 us
  waiting for transfers between devices: 96 us -> 146 us
  starting transfers between devices: 17.2 us -> 43 us
  local copies, waits for them, and re-layouts: 32.8 us -> 47.3 us
  other arithmetic: 6.47 us -> 10.1 us
    all_to_all x1 -> x0, blocking collectives: 82.2 us -> none  [per_device(): lax.all_to_all(block_rows, 'own', split_axis=0, concat_axis=0, tiled=True)]
    all_to_all x1 -> x4, waiting for transfers between devices: 93.9 us -> 144 us  [the longest x2 92.1 us: per_device(): lax.all_to_all(spread, 'own', split_axis=0, concat_axis=0, tiled=True)]
    all_to_all x1 -> x4, starting transfers between devices: 16.8 us -> 42.6 us  [the longest x2 25.9 us: per_device(): lax.all_to_all(spread, 'own', split_axis=0, concat_axis=0, tiled=True)]
    reshape x5 -> x9, local copies, waits for them, and re-layouts: 8.68 us -> 13 us  [the longest x2 6.04 us: per_device(): rows_cot = got[:, 8:].reshape(owners * chunk, model_width)]
    broadcast_in_dim x2 -> x4, local copies, waits for them, and re-layouts: 3.01 us -> 6.68 us  [per_device(): jnp.broadcast_to(both, (experts_here, SPLIT) + both.shape[2:])]
    reshape x1 -> x2, local copies, waits for them, and re-layouts: 4.64 us -> 7.1 us  [per_device(): block_rows = grad_rows.astype(jnp.bfloat16).reshape(owners, 16, -1)]
    unnamed x20 -> x40, local copies, waits for them, and re-layouts: 5.13 us -> 7.28 us
    slice x2 -> x5, local copies, waits for them, and re-layouts: 4.6 us -> 6.45 us  [the longest x2 4.26 us: per_device(): rows_cot = got[:, 8:].reshape(owners * chunk, model_width)]
  transfers between devices with their start and end apart: 5 -> 8, of which waited for: 1 -> 4; matrix products, arithmetic and copies ran while one was open for 11% -> 15% of each run, Pallas kernels for 0% -> 0%
where the time goes in v4:
time: 281 us; the launch traced here: 279 us
  waiting for transfers between devices  146 us (52%)
  local copies, waits for them, and re-layouts  47.3 us (17%)
  starting transfers between devices  43 us (15%)
  matrix products  17.9 us (6%)
  between operations  14.2 us (5%)
  other arithmetic  10.1 us (4%)
    all_to_all x2, waiting for transfers between devices, per_device(): lax.all_to_all(spread, 'own', split_axis=0, concat_axis=0, tiled=True)  92.1 us
    all_to_all x2, waiting for transfers between devices, per_device(): lax.all_to_all(block_rows, 'own', split_axis=0, concat_axis=0, tiled=True)  52.2 us
    all_to_all x2, starting transfers between devices, per_device(): lax.all_to_all(spread, 'own', split_axis=0, concat_axis=0, tiled=True)  25.9 us
    all_to_all x2, starting transfers between devices, per_device(): lax.all_to_all(block_rows, 'own', split_axis=0, concat_axis=0, tiled=True)  16.7 us
    unnamed x40, local copies, waits for them, and re-layouts  7.28 us
    reshape x2, local copies, waits for them, and re-layouts, per_device(): block_rows = grad_rows.astype(jnp.bfloat16).reshape(owners, 16, -1)  7.1 us
    broadcast_in_dim x4, local copies, waits for them, and re-layouts, per_device(): jnp.broadcast_to(both, (experts_here, SPLIT) + both.shape[2:])  6.68 us
    reshape x2, local copies, waits for them, and re-layouts, per_device(): rows_cot = got[:, 8:].reshape(owners * chunk, model_width)  6.04 us
  transfers between devices with their start and end apart: 8, of which 4 were waited for; matrix products, arithmetic and copies ran while one was open for 15% of the time, Pallas kernels for 0%

profile of v4, /device:TPU:6, one launch (start us, length us, event | category | flops | bytes accessed | tf_op | source)
XLA Modules:
  0.0 278.8 jit_solution(13100876167235178583)
XLA Ops:
  7.2 0.9 copy.12
  8.3 0.8 copy.16
  9.5 1.9 reduce-window.6
  11.8 5.0 %gather_fusion = f32[768]{0:T(1024)S(1)} fusion(f32[256]{0:T(256)S(1)} %copy-done.1, s32[1024]{0:T(1024)S(1)} %pad_clamp_fusion), kind=kCustom, calls=%fused_computation | custom fusion | bytes 9216 | tf_op jit(solution)/shard_map/jit(_take)/gather | solution.py:40
  17.9 1.0 fusion.22
  19.4 1.0 fusion.21
  20.7 0.8 broadcast_in_dim.45
  21.5 1.6 broadcast_in_dim.46
  23.1 16.6 %all-to-all-start.2 = ((bf16[64,16,960]{2,1,0:T(8,128)(2,1)}), bf16[64,16,960]{2,1,0:T(8,128)(2,1)S(1)}, u32[]{:S(2)}, u32[]{:S(2)}) async-start(bf16[64,16,960]{2,1,0:T(8,128)(2,1)} %bitcast.3), calls=%async_computation.2 | async-start | bytes 4194304 | tf_op jit(solution)/shard_map/all_to_all | solution.py:71
  39.8 0.7 all-gather.8.cloned.1.call-update
  40.5 1.4 pad_maximum_fusion.2
  41.9 1.6 broadcast_in_dim.43
  43.5 48.4 %all-to-all-done.2 = bf16[64,16,960]{2,1,0:T(8,128)(2,1)S(1)} async-done(((bf16[64,16,960]{2,1,0:T(8,128)(2,1)}), bf16[64,16,960]{2,1,0:T(8,128)(2,1)S(1)}, u32[]{:S(2)}, u32[]{:S(2)}) %all-to-all-start.2) | async-done | bytes 1966112 | tf_op jit(solution)/shard_map/all_to_all | solution.py:71
  91.9 2.6 broadcast_in_dim.44
  94.5 9.3 %all-to-all-start = ((bf16[64,16,960]{2,1,0:T(8,128)(2,1)}), bf16[64,16,960]{2,1,0:T(8,128)(2,1)}, u32[]{:S(2)}, u32[]{:S(2)}) async-start(bf16[64,16,960]{2,1,0:T(8,128)(2,1)} %bitcast.1), calls=%async_computation | async-start | bytes 4194304 | tf_op jit(solution)/shard_map/all_to_all | solution.py:71
  103.8 0.7 all-gather.6.cloned.1.call-update
  104.6 0.7 all-gather.4.cloned.1.call-update
  105.5 1.6 fusion.20
  107.1 3.5 %reshape.179 = bf16[192,2560]{1,0:T(8,128)(2,1)} reshape(bf16[64,8,960]{2,1,0:T(8,128)(2,1)} %get-tuple-element.8) | data formatting | bytes 1966080 | tf_op jit(solution)/shard_map/reshape | solution.py:76
  110.6 1.5 reshape.180
  112.1 43.7 %all-to-all-done = bf16[64,16,960]{2,1,0:T(8,128)(2,1)} async-done(((bf16[64,16,960]{2,1,0:T(8,128)(2,1)}), bf16[64,16,960]{2,1,0:T(8,128)(2,1)}, u32[]{:S(2)}, u32[]{:S(2)}) %all-to-all-start) | async-done | bytes 1966112 | tf_op jit(solution)/shard_map/all_to_all | solution.py:71
  155.9 2.7 fusion.19
  158.6 2.5 reshape.174
  161.1 2.7 reshape.175
  163.8 1.9 fusion.24
  165.8 2.0 fusion.23
  167.8 2.1 fusion.12
  169.8 2.2 multiply_convert_fusion.4
  173.2 0.8 copy-done.2
  174.6 0.7 copy-done.4
  177.3 0.8 copy-done.18
  178.0 0.6 multiply_convert_fusion.2
  179.8 2.1 pad_maximum_fusion
  181.9 1.3 copy-done.3
  184.1 1.4 fusion.3
  185.6 4.0 %reshape.176 = bf16[64,16,480]{2,1,0:T(8,128)(2,1)} reshape(bf16[192,2560]{1,0:T(8,128)(2,1)} %fusion.3) | data formatting | bytes 1966080 | tf_op jit(solution)/shard_map/reshape | solution.py:82
  189.6 10.0 %all-to-all-start.1 = ((bf16[64,16,480]{2,1,0:T(8,128)(2,1)}), bf16[64,16,480]{2,1,0:T(8,128)(2,1)}, u32[]{:S(2)}, u32[]{:S(2)}) async-start(bf16[64,16,480]{2,1,0:T(8,128)(2,1)} %reshape.176), calls=%async_computation.1 | async-start | bytes 2097152 | tf_op jit(solution)/shard_map/all_to_all | solution.py:83
  201.0 3.1 %reshape.181 = bf16[64,16,480]{2,1,0:T(8,128)(2,1)} reshape(bf16[192,2560]{1,0:T(8,128)(2,1)S(1)} %fusion.4) | data formatting | bytes 1966080 | tf_op jit(solution)/shard_map/reshape | solution.py:82
  204.0 25.4 %all-to-all-done.1 = bf16[64,16,480]{2,1,0:T(8,128)(2,1)} async-done(((bf16[64,16,480]{2,1,0:T(8,128)(2,1)}), bf16[64,16,480]{2,1,0:T(8,128)(2,1)}, u32[]{:S(2)}, u32[]{:S(2)}) %all-to-all-start.1) | async-done | bytes 983072 | tf_op jit(solution)/shard_map/all_to_all | solution.py:83
  229.4 6.8 %all-to-all-start.3 = ((bf16[64,16,480]{2,1,0:T(8,128)(2,1)}), bf16[64,16,480]{2,1,0:T(8,128)(2,1)S(1)}, u32[]{:S(2)}, u32[]{:S(2)}) async-start(bf16[64,16,480]{2,1,0:T(8,128)(2,1)} %reshape.181), calls=%async_computation.3 | async-start | bytes 2097152 | tf_op jit(solution)/shard_map/all_to_all | solution.py:83
  236.2 1.5 convert_reduce_fusion.1
  237.6 0.6 reshape.177
  238.3 26.8 %all-to-all-done.3 = bf16[64,16,480]{2,1,0:T(8,128)(2,1)S(1)} async-done(((bf16[64,16,480]{2,1,0:T(8,128)(2,1)}), bf16[64,16,480]{2,1,0:T(8,128)(2,1)S(1)}, u32[]{:S(2)}, u32[]{:S(2)}) %all-to-all-start.3) | async-done | bytes 983072 | tf_op jit(solution)/shard_map/all_to_all | solution.py:83
  265.1 1.0 convert_reduce_fusion
  266.1 1.7 reshape.182
  268.1 2.1 convolution_convert_fusion
  270.2 1.1 convert_element_type.81
  271.3 1.0 slice_bitcast_fusion
  (75 shorter events, 10.9 us)
Async XLA Ops:
  7.2 10.3 %copy-start = (bf16[128,2560]{1,0:T(8,128)(2,1)S(1)}, bf16[128,2560]{1,0:T(8,128)(2,1)}, u32[]{:S(2)}) copy-start(bf16[128,2560]{1,0:T(8,128)(2,1)} %param.9) | copy-start | bytes 1966084
  7.2 4.6 %copy-start.1 = (f32[256]{0:T(256)S(1)}, f32[256]{0:T(256)}, u32[]{:S(2)}) copy-start(f32[256]{0:T(256)} %param.12) | copy-start | bytes 3076
  17.8 1.1 copy-start.9
  23.1 68.7 %all-to-all-start.2 = ((bf16[64,16,960]{2,1,0:T(8,128)(2,1)}), bf16[64,16,960]{2,1,0:T(8,128)(2,1)S(1)}, u32[]{:S(2)}, u32[]{:S(2)}) async-start(bf16[64,16,960]{2,1,0:T(8,128)(2,1)} %bitcast.3), calls=%async_computation.2 | async-start | bytes 4194304 | tf_op jit(solution)/shard_map/all_to_all | solution.py:71
  39.7 124.1 %all-gather.8.cloned.1.call-start = ((), (), s32[]{:S(2)}) async-start(), calls=%async_computation.7 | async-start | bytes 1474560 | tf_op jit(solution)/shard_map/all_gather | solution.py:57
  94.5 61.4 %all-to-all-start = ((bf16[64,16,960]{2,1,0:T(8,128)(2,1)}), bf16[64,16,960]{2,1,0:T(8,128)(2,1)}, u32[]{:S(2)}, u32[]{:S(2)}) async-start(bf16[64,16,960]{2,1,0:T(8,128)(2,1)} %bitcast.1), calls=%async_computation | async-start | bytes 4194304 | tf_op jit(solution)/shard_map/all_to_all | solution.py:71
  103.8 62.0 %all-gather.6.cloned.1.call-start = ((), (), s32[]{:S(2)}) async-start(), calls=%async_computation.6 | async-start | bytes 1474560 | tf_op jit(solution)/shard_map/all_gather | solution.py:58
  104.5 65.3 %all-gather.4.cloned.1.call-start = ((), (), s32[]{:S(2)}) async-start(), calls=%async_computation.5 | async-start | bytes 1474560 | tf_op jit(solution)/shard_map/all_gather | solution.py:59
  105.3 164.9 %reduce-scatter.2.cloned.1.call-start = ((), (), s32[]{:S(2)}) async-start(), calls=%async_computation.8 | async-start | bytes 4423680 | tf_op jit(solution)/shard_map/reduce_scatter | solution.py:95
  107.1 3.5 %copy-start.6 = (bf16[64,8,960]{2,1,0:T(8,128)(2,1)S(1)}, bf16[64,8,960]{2,1,0:T(8,128)(2,1)}, u32[]{:S(2)}) copy-start(bf16[64,8,960]{2,1,0:T(8,128)(2,1)} %get-tuple-element.9) | copy-start | bytes 2949124
  165.8 2.0 copy-start.8
  172.0 0.6 copy-start.14
  172.0 0.7 copy-start.10
  172.7 1.3 copy-start.2
  174.0 1.3 copy-start.4
  174.0 2.1 copy-start.5
  175.3 1.4 copy-start.7
  176.7 1.3 copy-start.18
  178.6 0.6 copy-start.16
  178.6 0.7 copy-start.12
  181.9 1.3 copy-start.3
  181.9 1.3 copy-start.11
  183.2 0.9 copy-start.15
  189.6 10.0 %copy-start.13 = (bf16[192,256]{1,0:T(8,128)(2,1)S(1)}, bf16[192,256]{1,0:T(8,128)(2,1)}, u32[]{:S(2)}) copy-start(bf16[192,256]{1,0:T(8,128)(2,1)} %copy-done.12) | copy-start | bytes 294916
  189.6 39.8 %all-to-all-start.1 = ((bf16[64,16,480]{2,1,0:T(8,128)(2,1)}), bf16[64,16,480]{2,1,0:T(8,128)(2,1)}, u32[]{:S(2)}, u32[]{:S(2)}) async-start(bf16[64,16,480]{2,1,0:T(8,128)(2,1)} %reshape.176), calls=%async_computation.1 | async-start | bytes 2097152 | tf_op jit(solution)/shard_map/all_to_all | solution.py:83
  199.6 0.9 copy-start.17
  229.4 35.7 %all-to-all-start.3 = ((bf16[64,16,480]{2,1,0:T(8,128)(2,1)}), bf16[64,16,480]{2,1,0:T(8,128)(2,1)S(1)}, u32[]{:S(2)}, u32[]{:S(2)}) async-start(bf16[64,16,480]{2,1,0:T(8,128)(2,1)} %reshape.181), calls=%async_computation.3 | async-start | bytes 2097152 | tf_op jit(solution)/shard_map/all_to_all | solution.py:83
Sparse Core Ops, SparseCore 0:
  42.6 28.3 all-gather.7
  106.7 28.3 all-gather.5
  137.2 29.0 all-gather.3
  182.1 38.1 reduce-scatter.1

commit v5 on v3

--- a/solution.py
+++ b/solution.py
@@ -37,8 +37,9 @@
     is_named = (pair_route == column // CAP).astype(jnp.int32)
     earlier = jnp.cumsum(is_named, axis=0) - is_named
     hit = jnp.where(earlier == column % CAP, is_named, 0)
-    gate_values = jnp.take(gate_table, gate_index.reshape(-1), axis=0)
-    slot_gate = jnp.sum(jnp.where(hit > 0, gate_values[:, None], 0.0), axis=0)
+    slot_entry = jnp.sum(jnp.where(hit > 0, gate_index.reshape(-1)[:, None], 0), axis=0)
+    table_ids = jnp.arange(gate_table.shape[0], dtype=jnp.int32)[None, :]
+    slot_gate = jnp.sum(jnp.where(slot_entry[:, None] == table_ids, gate_table[None, :], 0.0), axis=1)
     select = hit.reshape(tok_count, choices_each, slots).sum(axis=1).astype(jnp.float32)
     return select, slot_gate
 

time: 269 us -> 264 us (0.981); the launches traced: 265 us -> 263 us
  local copies, waits for them, and re-layouts: 32.8 us -> 27.5 us
    gather x1 -> x0, local copies, waits for them, and re-layouts: 4.98 us -> none  [slot_tables(): gate_values = jnp.take(gate_table, gate_index.reshape(-1), axis=0)]
where the time goes in v5:
time: 264 us; the launch traced here: 263 us
  waiting for transfers between devices  97.5 us (37%)
  blocking collectives  84.5 us (32%)
  local copies, waits for them, and re-layouts  27.5 us (10%)
  starting transfers between devices  17.2 us (7%)
  matrix products  16.1 us (6%)
  between operations  14.1 us (5%)
  other arithmetic  6.62 us (3%)
    all_to_all x1, waiting for transfers between devices, per_device(): got = lax.all_to_all(spread, 'own', split_axis=0, concat_axis=0, tiled=True)  95.4 us
    all_to_all x1, blocking collectives, per_device(): lax.all_to_all(block_rows, 'own', split_axis=0, concat_axis=0, tiled=True)  84.5 us
    all_to_all x1, starting transfers between devices, per_device(): got = lax.all_to_all(spread, 'own', split_axis=0, concat_axis=0, tiled=True)  16.8 us
  transfers between devices with their start and end apart: 5, of which 1 were waited for; matrix products, arithmetic and copies ran while one was open for 11% of the time, Pallas kernels for 0%

profile of v5, /device:TPU:6, one launch (start us, length us, event | category | flops | bytes accessed | tf_op | source)
XLA Modules:
  0.0 263.3 jit_solution(2331992144414069854)
XLA Ops:
  7.2 0.9 copy.17
  8.1 0.1 eq.48
  8.2 0.1 eq.52
  8.4 1.9 reduce-window.6
  10.3 0.3 slice_reduce_fusion
  10.6 0.8 copy.21
  11.4 0.1 broadcast_in_dim.41
  11.6 0.3 select_reduce_fusion
  11.8 0.2 copy.20
  12.1 0.2 reduce_sum.36
  12.3 0.2 select_reduce_fusion.1
  12.4 0.3 fusion.4
  12.8 0.2 reshape.98
  13.0 0.1 copy-done.5
  13.1 0.3 convolution_convert_fusion.4
  13.4 0.2 reshape.97
  13.6 0.4 pad_maximum_fusion.1
  14.0 0.8 broadcast_in_dim.45
  14.9 2.2 broadcast_in_dim.46
  17.0 16.8 %all-to-all-start = ((bf16[64,16,1920]{2,1,0:T(8,128)(2,1)}), bf16[64,16,1920]{2,1,0:T(8,128)(2,1)}, u32[]{:S(2)}, u32[]{:S(2)}) async-start(bf16[64,16,1920]{2,1,0:T(8,128)(2,1)} %bitcast.52), calls=%async_computation | async-start | bytes 7864320 | tf_op jit(solution)/shard_map/all_to_all | solution.py:62
  33.9 0.7 all-gather.6.cloned.1.call-update
  34.7 0.7 all-gather.8.cloned.1.call-update
  35.4 0.7 all-gather.4.cloned.1.call-update
  36.1 0.2 reduce-scatter.2.cloned.1.call-start
  36.3 95.4 %all-to-all-done = bf16[64,16,1920]{2,1,0:T(8,128)(2,1)} async-done(((bf16[64,16,1920]{2,1,0:T(8,128)(2,1)}), bf16[64,16,1920]{2,1,0:T(8,128)(2,1)}, u32[]{:S(2)}, u32[]{:S(2)}) %all-to-all-start) | async-done | bytes 3932192 | tf_op jit(solution)/shard_map/all_to_all | solution.py:62
  131.7 4.3 %fusion.10 = (bf16[64,8,1920]{2,1,0:T(8,128)(2,1)}, bf16[64,8,1920]{2,1,0:T(8,128)(2,1)}) fusion(bf16[64,16,1920]{2,1,0:T(8,128)(2,1)} %all-to-all-done), kind=kLoop, calls=%fused_computation.41 | loop fusion | bytes 7864320 | tf_op jit(solution)/shard_map/slice | solution.py:64
  136.0 3.3 %reshape.101 = bf16[384,2560]{1,0:T(8,128)(2,1)S(1)} reshape(bf16[64,8,1920]{2,1,0:T(8,128)(2,1)} %get-tuple-element.7) | data formatting | bytes 3932160 | tf_op jit(solution)/shard_map/reshape | solution.py:63
  139.4 4.3 %reshape.100 = bf16[384,2560]{1,0:T(8,128)(2,1)} reshape(bf16[64,8,1920]{2,1,0:T(8,128)(2,1)} %get-tuple-element.6) | data formatting | bytes 3932160 | tf_op jit(solution)/shard_map/reshape | solution.py:64
  143.7 2.0 fusion.11
  145.8 2.2 fusion.12
  148.0 0.7 copy-done.7
  148.7 2.0 fusion.3
  150.7 2.8 %multiply_convert_fusion.1 = (bf16[384,256]{1,0:T(8,128)(2,1)S(1)}, bf16[384,256]{1,0:T(8,128)(2,1)S(1)}) fusion(f32[384,256]{1,0:T(8,128)} %copy-done.7, f32[384,256]{1,0:T(8,128)} %copy-done.6, bf16[384,2560]{1,0:T(8,128)(2,1)} %reshape.100, bf16[256,2560]{1,0:T(8,128)(2,1)} %all-gather.4.cloned.1.call-done), kind=kOutput, calls=%fused_computation.18 | convolution fusion | flops 504594432 | bytes 4456448 | tf_op jit(solution)/shard_map/dot_general | solution.py:20
  153.5 0.9 fusion.1
  154.4 0.9 fusion.2
  155.3 0.4 copy-done.2
  155.7 2.1 pad_maximum_fusion
  157.8 1.3 copy-done.4
  159.1 0.7 fusion.13
  159.8 0.6 copy-done.3
  160.4 2.0 fusion
  162.4 4.6 %reshape.102 = bf16[64,16,960]{2,1,0:T(8,128)(2,1)S(1)} reshape(bf16[384,2560]{1,0:T(8,128)(2,1)} %fusion) | data formatting | bytes 3932160 | tf_op jit(solution)/shard_map/reshape | solution.py:73
  167.1 84.5 %all_to_all.10 = bf16[64,16,960]{2,1,0:T(8,128)(2,1)S(1)} all-to-all(bf16[64,16,960]{2,1,0:T(8,128)(2,1)S(1)} %reshape.102), channel_id=1, replica_groups=mesh['own'=64,'rep'=8] {'own'}, dimensions={0} | all-to-all | bytes 3932160 | tf_op jit(solution)/shard_map/all_to_all | solution.py:74
  251.5 0.4 convert_reduce_fusion
  252.0 0.7 reshape.103
  252.7 2.1 convolution_convert_fusion.3
  254.7 1.1 convert_element_type.57
  255.8 1.0 slice_bitcast_fusion
  (25 shorter events, 0.4 us)
Async XLA Ops:
  7.2 5.3 %copy-start = (bf16[128,2560]{1,0:T(8,128)(2,1)S(1)}, bf16[128,2560]{1,0:T(8,128)(2,1)}, u32[]{:S(2)}) copy-start(bf16[128,2560]{1,0:T(8,128)(2,1)} %param.9) | copy-start | bytes 1966084
  8.4 3.8 %copy-start.8 = (f32[256]{0:T(256)S(1)}, f32[256]{0:T(256)}, u32[]{:S(2)}) copy-start(f32[256]{0:T(256)} %param.12) | copy-start | bytes 3076
  12.0 1.1 copy-start.5
  17.0 114.7 %all-to-all-start = ((bf16[64,16,1920]{2,1,0:T(8,128)(2,1)}), bf16[64,16,1920]{2,1,0:T(8,128)(2,1)}, u32[]{:S(2)}, u32[]{:S(2)}) async-start(bf16[64,16,1920]{2,1,0:T(8,128)(2,1)} %bitcast.52), calls=%async_computation | async-start | bytes 7864320 | tf_op jit(solution)/shard_map/all_to_all | solution.py:62
  33.9 109.8 %all-gather.6.cloned.1.call-start = ((), (), s32[]{:S(2)}) async-start(), calls=%async_computation.4 | async-start | bytes 1474560 | tf_op jit(solution)/shard_map/all_gather | solution.py:67
  34.6 111.1 %all-gather.8.cloned.1.call-start = ((), (), s32[]{:S(2)}) async-start(), calls=%async_computation.5 | async-start | bytes 1474560 | tf_op jit(solution)/shard_map/all_gather | solution.py:66
  35.4 115.3 %all-gather.4.cloned.1.call-start = ((), (), s32[]{:S(2)}) async-start(), calls=%async_computation.3 | async-start | bytes 1474560 | tf_op jit(solution)/shard_map/all_gather | solution.py:68
  36.1 218.6 %reduce-scatter.2.cloned.1.call-start = ((), (), s32[]{:S(2)}) async-start(), calls=%async_computation.6 | async-start | bytes 4423680 | tf_op jit(solution)/shard_map/reduce_scatter | solution.py:85
  145.7 2.2 copy-start.6
  145.8 2.9 %copy-start.1 = (bf16[384,2560]{1,0:T(8,128)(2,1)S(1)}, bf16[384,2560]{1,0:T(8,128)(2,1)}, u32[]{:S(2)}) copy-start(bf16[384,2560]{1,0:T(8,128)(2,1)} %reshape.100) | copy-start | bytes 5898244
  148.0 0.7 copy-start.7
  154.4 1.3 copy-start.2
  157.8 1.3 copy-start.4
  159.1 1.3 copy-start.3
Sparse Core Ops, SparseCore 0:
  36.8 28.2 all-gather.5
  67.3 29.0 all-gather.7
  98.5 29.0 all-gather.3
  157.9 60.5 reduce-scatter.1

commit v6 on v5

--- a/solution.py
+++ b/solution.py
@@ -81,9 +81,9 @@
     grad_tokens = jnp.dot(
         select, per_slot, precision=lax.Precision.HIGHEST, preferred_element_type=jnp.float32
     ).astype(jnp.bfloat16)
-    stacked = jnp.stack([grad_gate, grad_up, grad_down]).astype(jnp.bfloat16)
-    shares = lax.psum_scatter(stacked, "rep", scatter_dimension=1, tiled=True).astype(jnp.float32)
-    return (grad_tokens, shares[0], shares[1], shares[2])
+    partials = tuple(g.astype(jnp.bfloat16) for g in (grad_gate, grad_up, grad_down))
+    shares = lax.psum_scatter(partials, "rep", scatter_dimension=0, tiled=True)
+    return (grad_tokens,) + tuple(share.astype(jnp.float32) for share in shares)
 
 
 def solution(mesh):

time: 264 us -> 304 us (1.15)
  blocking collectives: 84.5 us -> 0 us
  waiting for transfers between devices: 97.5 us -> 181 us
  starting transfers between devices: 17.2 us -> 50.4 us
  matrix products: 16.1 us -> 19.7 us
  other arithmetic: 6.62 us -> 10.1 us
    all_to_all x1 -> x0, blocking collectives: 84.5 us -> none  [per_device(): lax.all_to_all(block_rows, 'own', split_axis=0, concat_axis=0, tiled=True)]
    reduce_scatter x1 -> x3, waiting for transfers between devices: 0.01 us -> 83.1 us  [per_device(): shares = lax.psum_scatter(partials, 'rep', scatter_dimension=0, tiled=True)]
    all_to_all x0 -> x1, starting transfers between devices: none -> 33.4 us  [per_device(): lax.all_to_all(block_rows, 'own', split_axis=0, concat_axis=0, tiled=True)]
    convert_element_type x1 -> x3, other arithmetic: 1.11 us -> 4.98 us  [per_device(): share.astype(jnp.float32)]
  transfers between devices with their start and end apart: 5 -> 8, of which waited for: 1 -> 4; matrix products, arithmetic and copies ran while one was open for 11% -> 13% of each run, Pallas kernels for 0% -> 0%
where the time goes in v6:
time: 304 us; the launch traced here: 300 us
  waiting for transfers between devices  181 us (60%)
  starting transfers between devices  50.4 us (17%)
  local copies, waits for them, and re-layouts  25 us (8%)
  matrix products  19.7 us (6%)
  between operations  14.4 us (5%)
  other arithmetic  10.1 us (3%)
    all_to_all x1, waiting for transfers between devices, per_device(): got = lax.all_to_all(spread, 'own', split_axis=0, concat_axis=0, tiled=True)  95.6 us
    reduce_scatter x3, waiting for transfers between devices, per_device(): shares = lax.psum_scatter(partials, 'rep', scatter_dimension=0, tiled=True)  83.1 us
    all_to_all x1, starting transfers between devices, per_device(): lax.all_to_all(block_rows, 'own', split_axis=0, concat_axis=0, tiled=True)  33.4 us
    all_to_all x1, starting transfers between devices, per_device(): got = lax.all_to_all(spread, 'own', split_axis=0, concat_axis=0, tiled=True)  16.8 us
  transfers between devices with their start and end apart: 8, of which 4 were waited for; matrix products, arithmetic and copies ran while one was open for 13% of the time, Pallas kernels for 0%

profile of v6, /device:TPU:6, one launch (start us, length us, event | category | flops | bytes accessed | tf_op | source)
XLA Modules:
  0.0 300.4 jit_solution(7789366348581806594)
XLA Ops:
  7.2 0.9 copy.17
  8.1 0.1 eq.48
  8.2 0.1 eq.52
  8.3 0.1 compare_convert_fusion
  8.4 1.9 reduce-window.6
  10.3 0.3 slice_reduce_fusion
  10.6 0.8 copy.21
  11.4 0.1 broadcast_in_dim.41
  11.6 0.3 select_reduce_fusion
  11.8 0.2 copy.20
  12.1 0.2 reduce_sum.36
  12.3 0.2 select_reduce_fusion.1
  12.4 0.3 fusion.1
  12.8 0.2 reshape.98
  13.0 0.1 copy-done.3
  13.1 0.3 convolution_convert_fusion.4
  13.4 0.2 reshape.97
  13.6 0.4 pad_maximum_fusion
  14.0 0.8 broadcast_in_dim.45
  14.9 2.2 broadcast_in_dim.46
  17.1 16.8 %all-to-all-start = ((bf16[64,16,1920]{2,1,0:T(8,128)(2,1)}), bf16[64,16,1920]{2,1,0:T(8,128)(2,1)}, u32[]{:S(2)}, u32[]{:S(2)}) async-start(bf16[64,16,1920]{2,1,0:T(8,128)(2,1)} %bitcast.40), calls=%async_computation | async-start | bytes 7864320 | tf_op jit(solution)/shard_map/all_to_all | solution.py:62
  33.9 0.7 all-gather.6.cloned.1.call-update
  34.7 0.7 all-gather.8.cloned.1.call-update
  35.4 0.7 all-gather.4.cloned.1.call-update
  36.2 95.6 %all-to-all-done = bf16[64,16,1920]{2,1,0:T(8,128)(2,1)} async-done(((bf16[64,16,1920]{2,1,0:T(8,128)(2,1)}), bf16[64,16,1920]{2,1,0:T(8,128)(2,1)}, u32[]{:S(2)}, u32[]{:S(2)}) %all-to-all-start) | async-done | bytes 3932192 | tf_op jit(solution)/shard_map/all_to_all | solution.py:62
  131.7 4.3 %fusion.7 = (bf16[64,8,1920]{2,1,0:T(8,128)(2,1)}, bf16[64,8,1920]{2,1,0:T(8,128)(2,1)}) fusion(bf16[64,16,1920]{2,1,0:T(8,128)(2,1)} %all-to-all-done), kind=kLoop, calls=%fused_computation.34 | loop fusion | bytes 7864320 | tf_op jit(solution)/shard_map/slice | solution.py:64
  136.0 3.3 %reshape.101 = bf16[384,2560]{1,0:T(8,128)(2,1)S(1)} reshape(bf16[64,8,1920]{2,1,0:T(8,128)(2,1)} %get-tuple-element.7) | data formatting | bytes 3932160 | tf_op jit(solution)/shard_map/reshape | solution.py:63
  139.4 4.3 %reshape.100 = bf16[384,2560]{1,0:T(8,128)(2,1)} reshape(bf16[64,8,1920]{2,1,0:T(8,128)(2,1)} %get-tuple-element.6) | data formatting | bytes 3932160 | tf_op jit(solution)/shard_map/reshape | solution.py:64
  143.7 2.0 fusion.8
  145.8 2.2 fusion.9
  148.0 0.7 copy-done.5
  148.7 2.0 convolution_convert_fusion
  150.8 2.8 multiply_convert_fusion.1
  153.6 2.0 convolution_convert_fusion.1
  155.6 2.1 fusion.10
  157.7 2.0 fusion
  159.7 5.5 %reshape.102 = bf16[64,16,960]{2,1,0:T(8,128)(2,1)} reshape(bf16[384,2560]{1,0:T(8,128)(2,1)} %fusion) | data formatting | bytes 3932160 | tf_op jit(solution)/shard_map/reshape | solution.py:73
  165.2 33.4 %all-to-all-start.1 = ((bf16[64,16,960]{2,1,0:T(8,128)(2,1)}), bf16[64,16,960]{2,1,0:T(8,128)(2,1)}, u32[]{:S(2)}, u32[]{:S(2)}) async-start(bf16[64,16,960]{2,1,0:T(8,128)(2,1)} %reshape.102), calls=%async_computation.1 | async-start | bytes 4194304 | tf_op jit(solution)/shard_map/all_to_all | solution.py:74
  198.6 1.9 convolution_convert_fusion.2
  200.6 6.3 %reduce-scatter.8.cloned.1.call-done = bf16[32,2560]{1,0:T(8,128)(2,1)} async-done(((bf16[256,2560]{1,0:T(8,128)(2,1)}), bf16[32,2560]{1,0:T(8,128)(2,1)}) %reduce-scatter.8.cloned.1.call-update) | async-done | bytes 163856 | tf_op jit(solution)/shard_map/reduce_scatter | solution.py:85
  206.9 1.7 convert_element_type.76
  208.5 39.0 %reduce-scatter.6.cloned.1.call-done = bf16[32,2560]{1,0:T(8,128)(2,1)} async-done(((bf16[256,2560]{1,0:T(8,128)(2,1)}), bf16[32,2560]{1,0:T(8,128)(2,1)}) %reduce-scatter.6.cloned.1.call-update) | async-done | bytes 163856 | tf_op jit(solution)/shard_map/reduce_scatter | solution.py:85
  247.5 1.7 convert_element_type.73
  249.1 37.8 %reduce-scatter.4.cloned.1.call-done = bf16[32,2560]{1,0:T(8,128)(2,1)} async-done(((bf16[256,2560]{1,0:T(8,128)(2,1)}), bf16[32,2560]{1,0:T(8,128)(2,1)}) %reduce-scatter.4.cloned.1.call-update) | async-done | bytes 163856 | tf_op jit(solution)/shard_map/reduce_scatter | solution.py:85
  287.0 1.7 convert_element_type.71
  288.7 2.1 convert_reduce_fusion
  290.8 0.7 reshape.103
  291.5 2.1 convolution_convert_fusion.3
  (28 shorter events, 0.5 us)
Async XLA Ops:
  7.2 5.3 %copy-start = (bf16[128,2560]{1,0:T(8,128)(2,1)S(1)}, bf16[128,2560]{1,0:T(8,128)(2,1)}, u32[]{:S(2)}) copy-start(bf16[128,2560]{1,0:T(8,128)(2,1)} %param.9) | copy-start | bytes 1966084
  8.4 3.8 %copy-start.6 = (f32[256]{0:T(256)S(1)}, f32[256]{0:T(256)}, u32[]{:S(2)}) copy-start(f32[256]{0:T(256)} %param.12) | copy-start | bytes 3076
  12.0 1.1 copy-start.3
  17.1 114.7 %all-to-all-start = ((bf16[64,16,1920]{2,1,0:T(8,128)(2,1)}), bf16[64,16,1920]{2,1,0:T(8,128)(2,1)}, u32[]{:S(2)}, u32[]{:S(2)}) async-start(bf16[64,16,1920]{2,1,0:T(8,128)(2,1)} %bitcast.40), calls=%async_computation | async-start | bytes 7864320 | tf_op jit(solution)/shard_map/all_to_all | solution.py:62
  33.9 109.8 %all-gather.6.cloned.1.call-start = ((), (), s32[]{:S(2)}) async-start(), calls=%async_computation.6 | async-start | bytes 1474560 | tf_op jit(solution)/shard_map/all_gather | solution.py:67
  34.6 111.1 %all-gather.8.cloned.1.call-start = ((), (), s32[]{:S(2)}) async-start(), calls=%async_computation.7 | async-start | bytes 1474560 | tf_op jit(solution)/shard_map/all_gather | solution.py:66
  35.4 115.4 %all-gather.4.cloned.1.call-start = ((), (), s32[]{:S(2)}) async-start(), calls=%async_computation.5 | async-start | bytes 1474560 | tf_op jit(solution)/shard_map/all_gather | solution.py:68
  36.1 170.8 %reduce-scatter.8.cloned.1.call-start = ((), (), s32[]{:S(2)}) async-start(), calls=%async_computation.10 | async-start | bytes 1474560 | tf_op jit(solution)/shard_map/reduce_scatter | solution.py:85
  145.7 2.2 copy-start.4
  145.8 3.0 copy-start.1
  148.0 0.7 copy-start.5
  150.7 96.8 %reduce-scatter.6.cloned.1.call-start = ((), (), s32[]{:S(2)}) async-start(), calls=%async_computation.9 | async-start | bytes 1474560 | tf_op jit(solution)/shard_map/reduce_scatter | solution.py:85
  155.6 2.1 copy-start.2
  165.2 123.4 %all-to-all-start.1 = ((bf16[64,16,960]{2,1,0:T(8,128)(2,1)}), bf16[64,16,960]{2,1,0:T(8,128)(2,1)}, u32[]{:S(2)}, u32[]{:S(2)}) async-start(bf16[64,16,960]{2,1,0:T(8,128)(2,1)} %reshape.102), calls=%async_computation.1 | async-start | bytes 4194304 | tf_op jit(solution)/shard_map/all_to_all | solution.py:74
  198.6 88.4 %reduce-scatter.4.cloned.1.call-start = ((), (), s32[]{:S(2)}) async-start(), calls=%async_computation.8 | async-start | bytes 1474560 | tf_op jit(solution)/shard_map/reduce_scatter | solution.py:85
Sparse Core Ops, SparseCore 0:
  36.8 28.2 all-gather.5
  67.3 29.0 all-gather.7
  98.5 29.0 all-gather.3
  150.8 55.9 reduce-scatter.7
  209.6 37.8 reduce-scatter.5
  250.2 36.7 reduce-scatter.3

commit v7 on v5

--- a/solution.py
+++ b/solution.py
@@ -82,8 +82,8 @@
         select, per_slot, precision=lax.Precision.HIGHEST, preferred_element_type=jnp.float32
     ).astype(jnp.bfloat16)
     stacked = jnp.stack([grad_gate, grad_up, grad_down]).astype(jnp.bfloat16)
-    shares = lax.psum_scatter(stacked, "rep", scatter_dimension=1, tiled=True).astype(jnp.float32)
-    return (grad_tokens, shares[0], shares[1], shares[2])
+    shares = lax.psum_scatter(stacked, "rep", scatter_dimension=1, tiled=True)
+    return (grad_tokens,) + tuple(shares[i].astype(jnp.float32) for i in range(3))
 
 
 def solution(mesh):

time: 264 us -> 264 us (level)
  no operation moved by 1% of the time
where the time goes in v7:
time: 264 us; the launch traced here: 263 us
  waiting for transfers between devices  97.5 us (37%)
  blocking collectives  84.5 us (32%)
  local copies, waits for them, and re-layouts  26.5 us (10%)
  starting transfers between devices  17.2 us (7%)
  matrix products  16.1 us (6%)
  between operations  14 us (5%)
  other arithmetic  7.54 us (3%)
    all_to_all x1, waiting for transfers between devices, per_device(): got = lax.all_to_all(spread, 'own', split_axis=0, concat_axis=0, tiled=True)  95.4 us
    all_to_all x1, blocking collectives, per_device(): lax.all_to_all(block_rows, 'own', split_axis=0, concat_axis=0, tiled=True)  84.5 us
    all_to_all x1, starting transfers between devices, per_device(): got = lax.all_to_all(spread, 'own', split_axis=0, concat_axis=0, tiled=True)  16.8 us
  transfers between devices with their start and end apart: 5, of which 1 were waited for; matrix products, arithmetic and copies ran while one was open for 11% of the time, Pallas kernels for 0%

profile of v7, /device:TPU:6, one launch (start us, length us, event | category | flops | bytes accessed | tf_op | source)
XLA Modules:
  0.0 263.3 jit_solution(13958767443239236424)
XLA Ops:
  7.2 0.9 copy.17
  8.1 0.1 eq.48
  8.2 0.1 eq.52
  8.3 0.1 compare_convert_fusion
  8.4 1.9 reduce-window.6
  10.3 0.3 slice_reduce_fusion
  10.6 0.8 copy.21
  11.4 0.1 broadcast_in_dim.41
  11.6 0.3 select_reduce_fusion
  11.8 0.2 copy.20
  12.1 0.2 reduce_sum.36
  12.3 0.2 select_reduce_fusion.1
  12.4 0.3 fusion.4
  12.8 0.2 reshape.104
  13.0 0.1 copy-done.5
  13.1 0.3 convolution_convert_fusion.4
  13.4 0.2 reshape.103
  13.6 0.4 pad_maximum_fusion.1
  14.0 0.8 broadcast_in_dim.45
  14.9 2.2 broadcast_in_dim.46
  17.0 16.8 %all-to-all-start = ((bf16[64,16,1920]{2,1,0:T(8,128)(2,1)}), bf16[64,16,1920]{2,1,0:T(8,128)(2,1)}, u32[]{:S(2)}, u32[]{:S(2)}) async-start(bf16[64,16,1920]{2,1,0:T(8,128)(2,1)} %bitcast.61), calls=%async_computation | async-start | bytes 7864320 | tf_op jit(solution)/shard_map/all_to_all | solution.py:62
  33.9 0.7 all-gather.6.cloned.1.call-update
  34.7 0.7 all-gather.8.cloned.1.call-update
  35.4 0.7 all-gather.4.cloned.1.call-update
  36.1 0.2 reduce-scatter.2.cloned.1.call-start
  36.3 95.4 %all-to-all-done = bf16[64,16,1920]{2,1,0:T(8,128)(2,1)} async-done(((bf16[64,16,1920]{2,1,0:T(8,128)(2,1)}), bf16[64,16,1920]{2,1,0:T(8,128)(2,1)}, u32[]{:S(2)}, u32[]{:S(2)}) %all-to-all-start) | async-done | bytes 3932192 | tf_op jit(solution)/shard_map/all_to_all | solution.py:62
  131.7 4.3 %fusion.13 = (bf16[64,8,1920]{2,1,0:T(8,128)(2,1)}, bf16[64,8,1920]{2,1,0:T(8,128)(2,1)}) fusion(bf16[64,16,1920]{2,1,0:T(8,128)(2,1)} %all-to-all-done), kind=kLoop, calls=%fused_computation.44 | loop fusion | bytes 7864320 | tf_op jit(solution)/shard_map/slice | solution.py:64
  136.0 3.3 %reshape.107 = bf16[384,2560]{1,0:T(8,128)(2,1)S(1)} reshape(bf16[64,8,1920]{2,1,0:T(8,128)(2,1)} %get-tuple-element.7) | data formatting | bytes 3932160 | tf_op jit(solution)/shard_map/reshape | solution.py:63
  139.4 4.3 %reshape.106 = bf16[384,2560]{1,0:T(8,128)(2,1)} reshape(bf16[64,8,1920]{2,1,0:T(8,128)(2,1)} %get-tuple-element.6) | data formatting | bytes 3932160 | tf_op jit(solution)/shard_map/reshape | solution.py:64
  143.7 2.0 fusion.14
  145.8 2.2 fusion.15
  148.0 0.7 copy-done.7
  148.7 2.0 fusion.3
  150.7 2.8 %multiply_convert_fusion.1 = (bf16[384,256]{1,0:T(8,128)(2,1)S(1)}, bf16[384,256]{1,0:T(8,128)(2,1)S(1)}) fusion(f32[384,256]{1,0:T(8,128)} %copy-done.7, f32[384,256]{1,0:T(8,128)} %copy-done.6, bf16[384,2560]{1,0:T(8,128)(2,1)} %reshape.106, bf16[256,2560]{1,0:T(8,128)(2,1)} %all-gather.4.cloned.1.call-done), kind=kOutput, calls=%fused_computation.18 | convolution fusion | flops 504594432 | bytes 4456448 | tf_op jit(solution)/shard_map/dot_general | solution.py:20
  153.5 0.9 fusion.1
  154.4 0.9 fusion.2
  155.3 0.4 copy-done.2
  155.7 2.1 pad_maximum_fusion
  157.8 1.3 copy-done.4
  159.1 0.7 fusion.16
  159.8 0.6 copy-done.3
  160.4 2.0 fusion
  162.4 4.6 %reshape.108 = bf16[64,16,960]{2,1,0:T(8,128)(2,1)S(1)} reshape(bf16[384,2560]{1,0:T(8,128)(2,1)} %fusion) | data formatting | bytes 3932160 | tf_op jit(solution)/shard_map/reshape | solution.py:73
  167.1 84.5 %all_to_all.10 = bf16[64,16,960]{2,1,0:T(8,128)(2,1)S(1)} all-to-all(bf16[64,16,960]{2,1,0:T(8,128)(2,1)S(1)} %reshape.108), channel_id=1, replica_groups=mesh['own'=64,'rep'=8] {'own'}, dimensions={0} | all-to-all | bytes 3932160 | tf_op jit(solution)/shard_map/all_to_all | solution.py:74
  251.5 0.4 convert_reduce_fusion
  252.0 0.7 reshape.109
  252.7 2.1 convolution_convert_fusion.3
  254.7 2.0 fusion.7
  (24 shorter events, 0.3 us)
Async XLA Ops:
  7.2 5.3 %copy-start = (bf16[128,2560]{1,0:T(8,128)(2,1)S(1)}, bf16[128,2560]{1,0:T(8,128)(2,1)}, u32[]{:S(2)}) copy-start(bf16[128,2560]{1,0:T(8,128)(2,1)} %param.9) | copy-start | bytes 1966084
  8.4 3.8 %copy-start.8 = (f32[256]{0:T(256)S(1)}, f32[256]{0:T(256)}, u32[]{:S(2)}) copy-start(f32[256]{0:T(256)} %param.12) | copy-start | bytes 3076
  12.0 1.1 copy-start.5
  17.0 114.7 %all-to-all-start = ((bf16[64,16,1920]{2,1,0:T(8,128)(2,1)}), bf16[64,16,1920]{2,1,0:T(8,128)(2,1)}, u32[]{:S(2)}, u32[]{:S(2)}) async-start(bf16[64,16,1920]{2,1,0:T(8,128)(2,1)} %bitcast.61), calls=%async_computation | async-start | bytes 7864320 | tf_op jit(solution)/shard_map/all_to_all | solution.py:62
  33.9 109.8 %all-gather.6.cloned.1.call-start = ((), (), s32[]{:S(2)}) async-start(), calls=%async_computation.4 | async-start | bytes 1474560 | tf_op jit(solution)/shard_map/all_gather | solution.py:67
  34.6 111.1 %all-gather.8.cloned.1.call-start = ((), (), s32[]{:S(2)}) async-start(), calls=%async_computation.5 | async-start | bytes 1474560 | tf_op jit(solution)/shard_map/all_gather | solution.py:66
  35.4 115.3 %all-gather.4.cloned.1.call-start = ((), (), s32[]{:S(2)}) async-start(), calls=%async_computation.3 | async-start | bytes 1474560 | tf_op jit(solution)/shard_map/all_gather | solution.py:68
  36.1 218.6 %reduce-scatter.2.cloned.1.call-start = ((), (), s32[]{:S(2)}) async-start(), calls=%async_computation.6 | async-start | bytes 4423680 | tf_op jit(solution)/shard_map/reduce_scatter | solution.py:85
  145.7 2.2 copy-start.6
  145.8 2.9 %copy-start.1 = (bf16[384,2560]{1,0:T(8,128)(2,1)S(1)}, bf16[384,2560]{1,0:T(8,128)(2,1)}, u32[]{:S(2)}) copy-start(bf16[384,2560]{1,0:T(8,128)(2,1)} %reshape.106) | copy-start | bytes 5898244
  148.0 0.7 copy-start.7
  154.4 1.3 copy-start.2
  157.8 1.3 copy-start.4
  159.1 1.3 copy-start.3
Sparse Core Ops, SparseCore 0:
  36.8 28.2 all-gather.5
  67.3 29.0 all-gather.7
  98.5 29.0 all-gather.3
  157.9 60.5 reduce-scatter.1
